TPU v7x, 768 devices: a whole 4x8x12 slice. The times are simulated.
768 devices in a mesh: dp: 96 (over x, z, core), zero: 8 (over y).
Axes of the slice: x: 4, y: 8, z: 12, core: 2. Of those that a mesh axis runs over, the one named last changes fastest.
Arguments:
- grad_parts: bfloat16 [96, 3, 704, 1024], P('dp', None, 'zero'), may hold values from -1.5 to 1.5
- momentum: float32 [3, 704, 1024], P(None, 'zero')
- owner_table: int32 [3], replicated, may hold values from 0 to 7, as said below
Outputs:
- new_momentum: float32 [3, 704, 1024], P(None, 'zero')
- update: bfloat16 [3, 704, 1024], P(None, 'zero')
- owner_copy: bfloat16 [8, 704, 1024], P('zero')
Inputs may be any that keep to these rules, and one draw needn't show every extreme that they name: `owner_table`: the 3 entries are distinct; the first and the last device along zero always own a matrix.
All inputs are finite; a program needn't handle non-finite values.
Results may differ from a plain program's by a relative error of at most 0.0062.
Values may be sent and summed in bfloat16 or wider, within the bound.
No kernel may reach another device: no remote copies, remote signals or barrier semaphores. Data moves between devices by JAX's collectives and lax.ppermute only.
A program may use at most 32 MiB of HBM per device.

v0:
```python
import math

import jax
import jax.numpy as jnp
from jax import lax
from jax.sharding import PartitionSpec as P

D = 1024
ITERS = 2


COEF_A = 3.4445
COEF_B = -4.775
COEF_C = 2.0315
MOMENTUM_DECAY = 0.95
NORM_EPSILON = 1e-07


def orthogonalize(matrix):
    current = matrix
    iterate = matrix.astype(jnp.float32)
    for step in range(ITERS):
        gram_matrix = jnp.dot(current, current.T, preferred_element_type=jnp.float32).astype(
            jnp.bfloat16
        )
        squared = jnp.dot(gram_matrix, gram_matrix, preferred_element_type=jnp.float32)
        poly_term = (COEF_B * gram_matrix.astype(jnp.float32) + COEF_C * squared).astype(
            jnp.bfloat16
        )
        iterate = COEF_A * current.astype(jnp.float32) + jnp.dot(
            poly_term, current, preferred_element_type=jnp.float32
        )
        if step + 1 < ITERS:
            current = iterate.astype(jnp.bfloat16)
    return (0.2 * math.sqrt(D) * iterate).astype(jnp.bfloat16)


def on_device(grad_parts, momentum, owner_table):
    my_index = lax.axis_index("zero")
    local_part = grad_parts[0].astype(jnp.float32)
    summed = lax.psum(local_part, "dp")
    new_momentum = MOMENTUM_DECAY * momentum + summed
    partial_value = jnp.sum(new_momentum * new_momentum, axis=(1, 2))
    squares = lax.psum(partial_value, "zero")
    inverse = 1.0 / (jnp.sqrt(squares) + NORM_EPSILON)
    start_rows = (new_momentum * inverse[:, None, None]).astype(jnp.bfloat16)
    mine_mask = (owner_table == my_index).astype(jnp.bfloat16)
    gathered = lax.all_gather(start_rows, "zero", axis=1, tiled=True)
    full_matrix = jnp.einsum(
        "j,jrd->rd", mine_mask, gathered, preferred_element_type=jnp.float32
    ).astype(jnp.bfloat16)
    result = orthogonalize(full_matrix)
    contrib = mine_mask.astype(jnp.float32)[:, None, None] * result.astype(jnp.float32)[None]
    update_rows = lax.psum_scatter(
        contrib.astype(jnp.bfloat16), "zero", scatter_dimension=1, tiled=True
    )
    return (new_momentum, update_rows, result[None])


def solution(mesh):
    placed = (P("dp", None, "zero", None), P(None, "zero", None), P())
    return jax.shard_map(
        on_device,
        mesh=mesh,
        in_specs=placed,
        out_specs=(P(None, "zero", None), P(None, "zero", None), P("zero", None, None)),
        check_vma=False,
    )
```

profile of v0, /device:TPU:1, one launch (start us, length us, event | category | flops | bytes accessed | tf_op | source)
XLA Modules:
  0.0 478.7 jit_solution(3051840183665358192)
XLA Ops:
  7.2 0.0 copy-start.1
  7.2 0.0 all-reduce.2.cloned.1.call-start
  7.2 2.2 bitcast_convert_fusion.3
  9.4 0.0 all-reduce.2.cloned.1.call-update
  9.5 0.0 all-gather.2.cloned.1.call-start
  9.5 288.7 %all-reduce.2.cloned.1.call-done = f32[3,88,1024]{2,1,0:T(8,128)} async-done(((f32[3,88,1024]{2,1,0:T(8,128)}), f32[3,88,1024]{2,1,0:T(8,128)}) %all-reduce.2.cloned.1.call-update) | async-done | bytes 1081360 | tf_op jit(solution)/shard_map/psum | solution.py:41
  298.2 0.0 copy-done.1
  298.2 1.5 multiply_reduce_fusion
  299.7 0.0 copy-start
  299.7 0.0 copy-start.2
  299.7 13.4 %psum.15 = f32[3]{0:T(128)S(1)} all-reduce(f32[3]{0:T(128)S(1)} %get-tuple-element.3), channel_id=1, replica_groups=mesh['dp'=96,'zero'=8] {'zero'}, use_global_device_ids=true, to_apply=%region_2.0 | all-reduce | flops 3 | bytes 24 | tf_op jit(solution)/shard_map/psum | solution.py:44
  313.1 1.0 multiply_convert_fusion.2
  314.0 0.0 all-gather.2.cloned.1.call-update
  314.1 0.0 reduce-scatter.4.cloned.1.call-start
  314.1 0.0 copy-done.2
  314.1 57.7 %all-gather.2.cloned.1.call-done = bf16[3,704,1024]{2,1,0:T(8,128)(2,1)} async-done(((bf16[3,88,1024]{2,1,0:T(8,128)(2,1)}), bf16[3,704,1024]{2,1,0:T(8,128)(2,1)}) %all-gather.2.cloned.1.call-update) | async-done | bytes 4325392 | tf_op jit(solution)/shard_map/all_gather | solution.py:48
  371.9 7.6 %fusion = bf16[1,704,1024]{2,0,1:T(2,128)(2,1)} fusion(bf16[3,704,1024]{2,1,0:T(8,128)(2,1)} %all-gather.2.cloned.1.call-done, s32[3]{0:T(128)S(1)} %copy-done.2, s32[]{:T(128)S(6)} %axis_index.12), kind=kOutput, calls=%fused_computation.1 | convolution fusion | flops 4325379 | bytes 5767184 | tf_op jit(solution)/shard_map/j,jrd->rd/dot_general | solution.py:49
  379.5 0.0 copy-done
  379.5 4.2 convolution_convert_fusion.1
  383.7 5.1 %add_convert_fusion = bf16[704,1024]{1,0:T(8,128)(2,1)S(1)} fusion(bf16[704,704]{1,0:T(8,128)(2,1)S(1)} %convolution_convert_fusion.1, bf16[1,704,1024]{2,0,1:T(2,128)(2,1)} %fusion), kind=kOutput, calls=%fused_computation.5 | convolution fusion | flops 1718210560 | bytes 3874816 | tf_op jit(solution)/shard_map/dot_general | solution.py:30
  388.9 0.0 copy-start.3
  388.9 1.1 copy-done.3
  390.0 2.3 convolution_convert_fusion
  392.3 6.1 %fusion.10 = (f32[704,1024]{1,0:T(8,128)S(1)}, bf16[704,1024]{1,0:T(8,128)(2,1)}) fusion(bf16[704,1024]{1,0:T(8,128)(2,1)} %copy-done.3, bf16[704,704]{1,0:T(8,128)(2,1)} %convolution_convert_fusion), kind=kOutput, calls=%fused_computation.24 | convolution fusion | flops 1719652352 | bytes 6758400 | tf_op jit(solution)/shard_map/dot_general | solution.py:30
  398.4 1.2 multiply_convert_fusion
  399.6 3.9 copy.8
  403.5 4.8 copy.10
  408.3 0.0 reduce-scatter.4.cloned.1.call-update
  408.3 60.9 %reduce-scatter.4.cloned.1.call-done = bf16[88,3072]{1,0:T(8,128)(2,1)} async-done(((bf16[704,3072]{1,0:T(8,128)(2,1)}), bf16[88,3072]{1,0:T(8,128)(2,1)}) %reduce-scatter.4.cloned.1.call-update) | async-done | bytes 540688
  469.2 1.9 reshape.15
  471.1 1.0 copy.9
  (2 shorter events, 0.0 us)
Async XLA Ops:
  7.2 291.0 %copy-start.1 = (f32[3,88,1024]{2,1,0:T(8,128)S(1)}, f32[3,88,1024]{2,1,0:T(8,128)}, u32[]{:S(2)}) copy-start(f32[3,88,1024]{2,1,0:T(8,128)} %param.4) | copy-start | bytes 3244036
  7.2 291.0 %all-reduce.2.cloned.1.call-start = ((), (), s32[]{:S(2)}) async-start(), calls=%async_computation.1 | async-start | bytes 2162688 | tf_op jit(solution)/shard_map/psum | solution.py:41
  9.5 362.4 %all-gather.2.cloned.1.call-start = ((), (), s32[]{:S(2)}) async-start(), calls=%async_computation.2 | async-start | bytes 4866048 | tf_op jit(solution)/shard_map/all_gather | solution.py:48
  299.7 79.8 %copy-start = (f32[3,88,1024]{2,1,0:T(8,128)}, f32[3,88,1024]{2,1,0:T(8,128)S(1)}, u32[]{:S(2)}) copy-start(f32[3,88,1024]{2,1,0:T(8,128)S(1)} %get-tuple-element.4) | copy-start | bytes 3244036
  299.7 14.4 %copy-start.2 = (s32[3]{0:T(128)S(1)}, s32[3]{0:T(128)}, u32[]{:S(2)}) copy-start(s32[3]{0:T(128)} %param.5) | copy-start | bytes 40
  314.1 155.2 %reduce-scatter.4.cloned.1.call-start = ((), (), s32[]{:S(2)}) async-start(), calls=%async_computation.3 | async-start | bytes 4866048
  388.9 1.1 copy-start.3
Sparse Core Ops, SparseCore 0:
  12.0 286.1 all-reduce.1
  314.2 57.6 all-gather.1
  408.4 60.7 reduce-scatter.3
where the time goes:
time: 479 us
  waiting for transfers between devices  407 us (85%)
  matrix products  25.4 us (5%)
  between operations  13.8 us (3%)
  blocking collectives  13.4 us (3%)
  local copies, waits for them, and re-layouts  12.7 us (3%)
  other arithmetic  5.94 us (1%)
    psum x1, waiting for transfers between devices, on_device(): summed = lax.psum(local_part, 'dp')  289 us
    unnamed x4, waiting for transfers between devices  61 us
    all_gather x1, waiting for transfers between devices, on_device(): gathered = lax.all_gather(start_rows, 'zero', axis=1, tiled=True)  57.7 us
    psum x1, blocking collectives, on_device(): squares = lax.psum(partial_value, 'zero')  13.4 us
    unnamed x12, local copies, waits for them, and re-layouts  12.7 us
    dot_general x2, matrix products, orthogonalize(): jnp.dot(poly_term, current, preferred_element_type=jnp.float32)  11.2 us
  transfers between devices with their start and end apart: 3, of which 3 were waited for; matrix products, arithmetic and copies ran while one was open for 0% of the time, Pallas kernels for 0%

commit v1 on v0

--- a/solution.py
+++ b/solution.py
@@ -37,9 +37,16 @@
 
 def on_device(grad_parts, momentum, owner_table):
     my_index = lax.axis_index("zero")
-    local_part = grad_parts[0].astype(jnp.float32)
-    summed = lax.psum(local_part, "dp")
-    new_momentum = MOMENTUM_DECAY * momentum + summed
+    n_dp = lax.axis_size("dp")
+    local_part = grad_parts[0]
+    chunk = local_part.size // n_dp
+    pieces = lax.all_to_all(local_part.reshape(n_dp, chunk), "dp", 0, 0, tiled=True)
+    summed_chunk = jnp.sum(pieces.astype(jnp.float32), axis=0, keepdims=True)
+    dp_index = lax.axis_index("dp")
+    momentum_chunk = lax.dynamic_slice_in_dim(momentum.reshape(n_dp, chunk), dp_index, 1, 0)
+    new_chunk = MOMENTUM_DECAY * momentum_chunk + summed_chunk
+    spread = jnp.broadcast_to(new_chunk, (n_dp, chunk))
+    new_momentum = lax.all_to_all(spread, "dp", 0, 0, tiled=True).reshape(momentum.shape)
     partial_value = jnp.sum(new_momentum * new_momentum, axis=(1, 2))
     squares = lax.psum(partial_value, "zero")
     inverse = 1.0 / (jnp.sqrt(squares) + NORM_EPSILON)

time: 479 us -> 293 us (0.61)
  waiting for transfers between devices: 407 us -> 144 us
  blocking collectives: 13.4 us -> 62.8 us
  starting transfers between devices: 0.12 us -> 20.1 us
    psum x1 -> x0, waiting for transfers between devices: 289 us -> none  [on_device(): summed = lax.psum(local_part, 'dp')]
    all_to_all x0 -> x1, blocking collectives: none -> 48.8 us  [on_device(): lax.all_to_all(spread, 'dp', 0, 0, tiled=True).reshape(momentum.shape)]
    all_to_all x0 -> x1, waiting for transfers between devices: none -> 25.4 us  [on_device(): lax.all_to_all(local_part.reshape(n_dp, chunk), 'dp', 0, 0, tiled=True)]
    all_to_all x0 -> x1, starting transfers between devices: none -> 20 us  [on_device(): lax.all_to_all(local_part.reshape(n_dp, chunk), 'dp', 0, 0, tiled=True)]
    all_to_all x0 -> x2, other arithmetic: none -> 6.46 us  [the longest x1 3.89 us: on_device(): lax.all_to_all(local_part.reshape(n_dp, chunk), 'dp', 0, 0, tiled=True)]
    unnamed x4 -> x3, waiting for transfers between devices: 61 us -> 61 us
where the time goes in v1:
time: 293 us; the launch traced here: 292 us
  waiting for transfers between devices  144 us (49%)
  blocking collectives  62.8 us (21%)
  matrix products  24.6 us (8%)
  starting transfers between devices  20.1 us (7%)
  local copies, waits for them, and re-layouts  16.9 us (6%)
  between operations  14.2 us (5%)
  other arithmetic  9.95 us (3%)
    unnamed x3, waiting for transfers between devices  61 us
    all_gather x1, waiting for transfers between devices, on_device(): gathered = lax.all_gather(start_rows, 'zero', axis=1, tiled=True)  57.5 us
    all_to_all x1, blocking collectives, on_device(): lax.all_to_all(spread, 'dp', 0, 0, tiled=True).reshape(momentum.shape)  48.8 us
    all_to_all x1, waiting for transfers between devices, on_device(): lax.all_to_all(local_part.reshape(n_dp, chunk), 'dp', 0, 0, tiled=True)  25.4 us
    all_to_all x1, starting transfers between devices, on_device(): lax.all_to_all(local_part.reshape(n_dp, chunk), 'dp', 0, 0, tiled=True)  20 us
    psum x1, blocking collectives, on_device(): squares = lax.psum(partial_value, 'zero')  14.1 us
    unnamed x12, local copies, waits for them, and re-layouts  13 us
    dot_general x2, matrix products, orthogonalize(): jnp.dot(poly_term, current, preferred_element_type=jnp.float32)  11.9 us
  transfers between devices with their start and end apart: 3, of which 3 were waited for; matrix products, arithmetic and copies ran while one was open for 0% of the time, Pallas kernels for 0%

profile of v1, /device:TPU:1, one launch (start us, length us, event | category | flops | bytes accessed | tf_op | source)
XLA Modules:
  0.0 292.4 jit_solution(4488638292342608386)
XLA Ops:
  7.2 2.1 all_to_all.13
  9.3 0.5 broadcast.49
  9.8 3.9 %reduce.4 = bf16[96,2816]{1,0:T(8,128)(2,1)S(1)} reduce(bf16[96,1,2816]{2,1,0:T(2,128)(2,1)S(1)} %all_to_all.13, bf16[]{:T(256)} %broadcast.49), dimensions={1}, to_apply=%all_to_all.13.reduce_sub_computation | reduce | bytes 1081346 | tf_op jit(solution)/shard_map/all_to_all | solution.py:43
  13.7 0.0 copy-start.1
  13.7 0.9 reshape.34
  14.6 20.0 %all-to-all-start = ((bf16[96,2,1408]{2,1,0:T(2,128)(2,1)}), bf16[96,2,1408]{2,1,0:T(2,128)(2,1)S(1)}, u32[]{:S(2)}, u32[]{:S(2)}) async-start(bf16[96,2,1408]{2,1,0:T(2,128)(2,1)} %reshape.34), calls=%async_computation | async-start | bytes 1081344 | tf_op jit(solution)/shard_map/all_to_all | solution.py:43
  34.7 0.0 all-gather.2.cloned.1.call-start
  34.7 0.0 copy-done.1
  34.7 0.4 reshape.26
  35.1 25.4 %all-to-all-done = bf16[96,2,1408]{2,1,0:T(2,128)(2,1)S(1)} async-done(((bf16[96,2,1408]{2,1,0:T(2,128)(2,1)}), bf16[96,2,1408]{2,1,0:T(2,128)(2,1)S(1)}, u32[]{:S(2)}, u32[]{:S(2)}) %all-to-all-start) | async-done | bytes 540704 | tf_op jit(solution)/shard_map/all_to_all | solution.py:43
  60.5 0.4 reshape.35
  61.0 1.0 convert_reduce_fusion
  62.1 0.6 broadcast_in_dim.7
  62.6 48.8 %all_to_all.16 = f32[96,1,2816]{2,1,0:T(1,128)S(1)} all-to-all(f32[96,1,2816]{2,1,0:T(1,128)S(1)} %broadcast_in_dim.7), channel_id=1, replica_groups=mesh['dp'=96,'zero'=8] {'dp'}, dimensions={0} | all-to-all | bytes 2162688 | tf_op jit(solution)/shard_map/all_to_all | solution.py:49
  111.4 2.6 reduce.2
  114.0 0.3 reshape.27
  114.3 0.0 copy-start
  114.3 0.0 copy-start.2
  114.3 0.2 multiply_reduce_fusion
  114.5 14.1 %psum.7 = f32[3]{0:T(128)S(1)} all-reduce(f32[3]{0:T(128)S(1)} %multiply_reduce_fusion), channel_id=1, replica_groups=mesh['dp'=96,'zero'=8] {'zero'}, use_global_device_ids=true, to_apply=%region_2.0 | all-reduce | flops 3 | bytes 24 | tf_op jit(solution)/shard_map/psum | solution.py:51
  128.6 1.0 multiply_convert_fusion.2
  129.5 0.0 all-gather.2.cloned.1.call-update
  129.6 0.0 copy-done
  129.6 0.0 reduce-scatter.4.cloned.1.call-start
  129.6 0.0 copy-done.2
  129.6 57.5 %all-gather.2.cloned.1.call-done = bf16[3,704,1024]{2,1,0:T(8,128)(2,1)} async-done(((bf16[3,88,1024]{2,1,0:T(8,128)(2,1)}), bf16[3,704,1024]{2,1,0:T(8,128)(2,1)}) %all-gather.2.cloned.1.call-update) | async-done | bytes 4325392 | tf_op jit(solution)/shard_map/all_gather | solution.py:55
  187.1 6.0 %fusion = bf16[1,704,1024]{2,0,1:T(2,128)(2,1)S(1)} fusion(bf16[3,704,1024]{2,1,0:T(8,128)(2,1)} %all-gather.2.cloned.1.call-done, s32[3]{0:T(128)S(1)} %copy-done.2, s32[]{:T(128)S(6)} %axis_index.25), kind=kOutput, calls=%fused_computation.1 | convolution fusion | flops 4325379 | bytes 5767184 | tf_op jit(solution)/shard_map/j,jrd->rd/dot_general | solution.py:56
  193.2 2.5 convolution_convert_fusion.1
  195.7 5.7 %add_convert_fusion = bf16[704,1024]{1,0:T(8,128)(2,1)} fusion(bf16[704,704]{1,0:T(8,128)(2,1)} %convolution_convert_fusion.1, bf16[1,704,1024]{2,0,1:T(2,128)(2,1)S(1)} %fusion), kind=kOutput, calls=%fused_computation.5 | convolution fusion | flops 1718210560 | bytes 3874816 | tf_op jit(solution)/shard_map/dot_general | solution.py:30
  201.4 4.1 %convolution_convert_fusion = bf16[704,704]{1,0:T(8,128)(2,1)} fusion(bf16[704,1024]{1,0:T(8,128)(2,1)} %add_convert_fusion), kind=kOutput, calls=%fused_computation.8 | convolution fusion | flops 1015517184 | bytes 2433024 | tf_op jit(solution)/shard_map/dot_general | solution.py:23
  205.6 6.2 %fusion.10 = (f32[704,1024]{1,0:T(8,128)S(1)}, bf16[704,1024]{1,0:T(8,128)(2,1)}) fusion(bf16[704,1024]{1,0:T(8,128)(2,1)} %add_convert_fusion, bf16[704,704]{1,0:T(8,128)(2,1)} %convolution_convert_fusion), kind=kOutput, calls=%fused_computation.24 | convolution fusion | flops 1719652352 | bytes 6758400 | tf_op jit(solution)/shard_map/dot_general | solution.py:30
  211.8 1.2 multiply_convert_fusion
  213.0 3.9 %copy.9 = bf16[3,704,1024]{2,0,1:T(4,128)(2,1)S(1)} copy(bf16[3,704,1024]{2,1,0:T(8,128)(2,1)S(1)} %multiply_convert_fusion) | data formatting | bytes 8650752
  216.9 4.8 %copy.11 = bf16[88,8,3,1024]{3,1,2,0:T(8,128)(2,1)} copy(bf16[88,8,3,1024]{3,2,1,0:T(4,128)(2,1)S(1)} %bitcast.24) | data formatting | bytes 8650752
  221.7 0.0 reduce-scatter.4.cloned.1.call-update
  221.7 61.0 %reduce-scatter.4.cloned.1.call-done = bf16[88,3072]{1,0:T(8,128)(2,1)} async-done(((bf16[704,3072]{1,0:T(8,128)(2,1)}), bf16[88,3072]{1,0:T(8,128)(2,1)}) %reduce-scatter.4.cloned.1.call-update) | async-done | bytes 540688
  282.7 1.9 reshape.31
  284.6 1.0 copy.10
  (3 shorter events, 0.1 us)
Async XLA Ops:
  13.7 21.0 %copy-start.1 = (f32[3,88,1024]{2,1,0:T(8,128)S(1)}, f32[3,88,1024]{2,1,0:T(8,128)}, u32[]{:S(2)}) copy-start(f32[3,88,1024]{2,1,0:T(8,128)} %param.4) | copy-start | bytes 3244036
  14.6 45.9 %all-to-all-start = ((bf16[96,2,1408]{2,1,0:T(2,128)(2,1)}), bf16[96,2,1408]{2,1,0:T(2,128)(2,1)S(1)}, u32[]{:S(2)}, u32[]{:S(2)}) async-start(bf16[96,2,1408]{2,1,0:T(2,128)(2,1)} %reshape.34), calls=%async_computation | async-start | bytes 1081344 | tf_op jit(solution)/shard_map/all_to_all | solution.py:43
  34.7 152.5 %all-gather.2.cloned.1.call-start = ((), (), s32[]{:S(2)}) async-start(), calls=%async_computation.3 | async-start | bytes 4866048 | tf_op jit(solution)/shard_map/all_gather | solution.py:55
  114.3 15.3 %copy-start = (f32[3,88,1024]{2,1,0:T(8,128)}, f32[3,88,1024]{2,1,0:T(8,128)S(1)}, u32[]{:S(2)}) copy-start(f32[3,88,1024]{2,1,0:T(8,128)S(1)} %reshape.27) | copy-start | bytes 3244036
  114.3 15.4 %copy-start.2 = (s32[3]{0:T(128)S(1)}, s32[3]{0:T(128)}, u32[]{:S(2)}) copy-start(s32[3]{0:T(128)} %param.5) | copy-start | bytes 40
  129.6 153.1 %reduce-scatter.4.cloned.1.call-start = ((), (), s32[]{:S(2)}) async-start(), calls=%async_computation.4 | async-start | bytes 4866048
Sparse Core Ops, SparseCore 0:
  129.7 57.3 all-gather.1
  221.8 60.7 reduce-scatter.3

commit v2 on v1

--- a/solution.py
+++ b/solution.py
@@ -51,15 +51,18 @@
     squares = lax.psum(partial_value, "zero")
     inverse = 1.0 / (jnp.sqrt(squares) + NORM_EPSILON)
     start_rows = (new_momentum * inverse[:, None, None]).astype(jnp.bfloat16)
-    mine_mask = (owner_table == my_index).astype(jnp.bfloat16)
-    gathered = lax.all_gather(start_rows, "zero", axis=1, tiled=True)
-    full_matrix = jnp.einsum(
-        "j,jrd->rd", mine_mask, gathered, preferred_element_type=jnp.float32
-    ).astype(jnp.bfloat16)
+    n_zero = lax.axis_size("zero")
+    outgoing = jnp.zeros((n_zero,) + start_rows.shape[1:], start_rows.dtype)
+    owners = jnp.arange(n_zero, dtype=owner_table.dtype)[:, None, None]
+    for j in range(start_rows.shape[0]):
+        outgoing = jnp.where(owners == owner_table[j], start_rows[j][None], outgoing)
+    incoming = lax.all_to_all(outgoing, "zero", 0, 0, tiled=True)
+    full_matrix = incoming.reshape(-1, incoming.shape[-1])
     result = orthogonalize(full_matrix)
-    contrib = mine_mask.astype(jnp.float32)[:, None, None] * result.astype(jnp.float32)[None]
-    update_rows = lax.psum_scatter(
-        contrib.astype(jnp.bfloat16), "zero", scatter_dimension=1, tiled=True
+    returned = lax.all_to_all(result.reshape(incoming.shape), "zero", 0, 0, tiled=True)
+    update_rows = jnp.stack(
+        [lax.dynamic_index_in_dim(returned, owner_table[j], 0, keepdims=False)
+         for j in range(start_rows.shape[0])]
     )
     return (new_momentum, update_rows, result[None])
 

time: 293 us -> 214 us (0.73)
  the two profiles are of different devices: /device:TPU:1 before, /device:TPU:64 now
where the time goes in v2:
time: 214 us
  waiting for transfers between devices  94.1 us (44%)
  blocking collectives  55.4 us (26%)
  starting transfers between devices  28.3 us (13%)
  matrix products  11.3 us (5%)
  other arithmetic  11.1 us (5%)
  local copies, waits for them, and re-layouts  6.91 us (3%)
  between operations  6.51 us (3%)
    all_to_all x1, waiting for transfers between devices, on_device(): lax.all_to_all(spread, 'dp', 0, 0, tiled=True).reshape(momentum.shape)  40.8 us
    all_to_all x1, blocking collectives, on_device(): incoming = lax.all_to_all(outgoing, 'zero', 0, 0, tiled=True)  37.8 us
    all_to_all x1, waiting for transfers between devices, on_device(): lax.all_to_all(result.reshape(incoming.shape), 'zero', 0, 0, tiled=True)  26.8 us
    all_to_all x1, waiting for transfers between devices, on_device(): lax.all_to_all(local_part.reshape(n_dp, chunk), 'dp', 0, 0, tiled=True)  26.5 us
    all_to_all x1, starting transfers between devices, on_device(): lax.all_to_all(local_part.reshape(n_dp, chunk), 'dp', 0, 0, tiled=True)  18.2 us
    psum x1, blocking collectives, on_device(): squares = lax.psum(partial_value, 'zero')  17.6 us
    dot_general x2, matrix products, orthogonalize(): jnp.dot(poly_term, current, preferred_element_type=jnp.float32)  7.64 us
    all_to_all x1, starting transfers between devices, on_device(): lax.all_to_all(spread, 'dp', 0, 0, tiled=True).reshape(momentum.shape)  6.55 us
  transfers between devices with their start and end apart: 3, of which 3 were waited for; matrix products, arithmetic and copies ran while one was open for 1% of the time, Pallas kernels for 0%

profile of v2, /device:TPU:64, one launch (start us, length us, event | category | flops | bytes accessed | tf_op | source)
XLA Modules:
  0.0 213.6 jit_solution(13855015161864607269)
XLA Ops:
  0.6 2.1 all_to_all.21
  2.8 0.5 broadcast.58
  3.3 3.9 %reduce.4 = bf16[96,2816]{1,0:T(8,128)(2,1)S(1)} reduce(bf16[96,1,2816]{2,1,0:T(2,128)(2,1)S(1)} %all_to_all.21, bf16[]{:T(256)} %broadcast.58), dimensions={1}, to_apply=%all_to_all.21.reduce_sub_computation | reduce | bytes 1081346 | tf_op jit(solution)/shard_map/all_to_all | solution.py:43
  7.2 0.0 copy-start.1
  7.2 0.9 reshape.51
  8.1 18.2 %all-to-all-start = ((bf16[96,2,1408]{2,1,0:T(2,128)(2,1)}), bf16[96,2,1408]{2,1,0:T(2,128)(2,1)S(1)}, u32[]{:S(2)}, u32[]{:S(2)}) async-start(bf16[96,2,1408]{2,1,0:T(2,128)(2,1)} %reshape.51), calls=%async_computation | async-start | bytes 1081344 | tf_op jit(solution)/shard_map/all_to_all | solution.py:43
  26.3 0.0 copy-done.1
  26.3 0.4 reshape.45
  26.7 26.5 %all-to-all-done = bf16[96,2,1408]{2,1,0:T(2,128)(2,1)S(1)} async-done(((bf16[96,2,1408]{2,1,0:T(2,128)(2,1)}), bf16[96,2,1408]{2,1,0:T(2,128)(2,1)S(1)}, u32[]{:S(2)}, u32[]{:S(2)}) %all-to-all-start) | async-done | bytes 540704 | tf_op jit(solution)/shard_map/all_to_all | solution.py:43
  53.2 0.4 reshape.52
  53.6 1.0 convert_reduce_fusion
  54.7 0.0 copy-start.2
  54.7 1.5 broadcast_in_dim.59
  56.3 6.5 %all-to-all-start.1 = ((f32[96,1,2816]{2,1,0:T(1,128)}), f32[96,1,2816]{2,1,0:T(1,128)S(1)}, u32[]{:S(2)}, u32[]{:S(2)}) async-start(f32[96,1,2816]{2,1,0:T(1,128)} %broadcast_in_dim.59), calls=%async_computation.1 | async-start | bytes 2162688 | tf_op jit(solution)/shard_map/all_to_all | solution.py:49
  62.8 0.0 copy-done.2
  62.8 0.6 fusion.4
  63.4 1.3 iota_compare_fusion
  64.7 40.8 %all-to-all-done.1 = f32[96,1,2816]{2,1,0:T(1,128)S(1)} async-done(((f32[96,1,2816]{2,1,0:T(1,128)}), f32[96,1,2816]{2,1,0:T(1,128)S(1)}, u32[]{:S(2)}, u32[]{:S(2)}) %all-to-all-start.1) | async-done | bytes 1081376 | tf_op jit(solution)/shard_map/all_to_all | solution.py:49
  105.5 2.7 %reduce.2 = f32[96,2816]{1,0:T(8,128)S(1)} reduce(f32[96,1,2816]{2,1,0:T(1,128)S(1)} %all-to-all-done.1, f32[]{:T(128)} %constant.37), dimensions={1}, to_apply=%all_to_all.18.reduce_sub_computation | reduce | bytes 2162692 | tf_op jit(solution)/shard_map/all_to_all | solution.py:49
  108.2 0.3 reshape.46
  108.5 0.0 copy-start
  108.5 0.2 multiply_reduce_fusion
  108.7 0.7 iota_compare_fusion.2
  109.4 17.6 %psum.7 = f32[3]{0:T(128)S(1)} all-reduce(f32[3]{0:T(128)S(1)} %multiply_reduce_fusion), channel_id=1, replica_groups=mesh['dp'=96,'zero'=8] {'zero'}, use_global_device_ids=true, to_apply=%region_2.0 | all-reduce | flops 3 | bytes 24 | tf_op jit(solution)/shard_map/psum | solution.py:51
  127.0 0.2 multiply_convert_fusion.1
  127.2 0.0 copy-done
  127.2 0.3 select_select_fusion
  127.6 37.8 %all_to_all.26 = bf16[8,88,1024]{2,1,0:T(8,128)(2,1)S(1)} all-to-all(bf16[8,88,1024]{2,1,0:T(8,128)(2,1)S(1)} %select_select_fusion), channel_id=1, replica_groups=mesh['dp'=96,'zero'=8] {'zero'}, dimensions={0} | all-to-all | bytes 2883584 | tf_op jit(solution)/shard_map/all_to_all | solution.py:59
  165.3 2.3 %convolution_convert_fusion.1 = bf16[704,704]{1,0:T(8,128)(2,1)} fusion(bf16[704,1024]{1,0:T(8,128)(2,1)S(1)} %bitcast.24), kind=kOutput, calls=%fused_computation.5 | convolution fusion | flops 1015517184 | bytes 2433024 | tf_op jit(solution)/shard_map/dot_general | solution.py:23
  167.6 4.4 %add_convert_fusion = bf16[704,1024]{1,0:T(8,128)(2,1)S(1)} fusion(bf16[704,1024]{1,0:T(8,128)(2,1)S(1)} %bitcast.25, bf16[704,704]{1,0:T(8,128)(2,1)} %convolution_convert_fusion.1), kind=kOutput, calls=%fused_computation.1 | convolution fusion | flops 1718210560 | bytes 3874816 | tf_op jit(solution)/shard_map/dot_general | solution.py:30
  172.0 1.3 convolution_convert_fusion
  173.3 3.3 %multiply_convert_fusion = bf16[704,1024]{1,0:T(8,128)(2,1)} fusion(bf16[704,1024]{1,0:T(8,128)(2,1)S(1)} %add_convert_fusion, bf16[704,704]{1,0:T(8,128)(2,1)S(1)} %convolution_convert_fusion), kind=kOutput, calls=%fused_computation | convolution fusion | flops 1718931456 | bytes 3874816 | tf_op jit(solution)/shard_map/dot_general | solution.py:30
  176.6 3.6 %all-to-all-start.3 = ((bf16[8,88,1024]{2,1,0:T(8,128)(2,1)}), bf16[8,88,1024]{2,1,0:T(8,128)(2,1)S(1)}, u32[]{:S(2)}, u32[]{:S(2)}) async-start(bf16[8,88,1024]{2,1,0:T(8,128)(2,1)} %bitcast.7), calls=%async_computation.3 | async-start | bytes 2883584 | tf_op jit(solution)/shard_map/all_to_all | solution.py:62
  185.9 26.8 %all-to-all-done.3 = bf16[8,88,1024]{2,1,0:T(8,128)(2,1)S(1)} async-done(((bf16[8,88,1024]{2,1,0:T(8,128)(2,1)}), bf16[8,88,1024]{2,1,0:T(8,128)(2,1)S(1)}, u32[]{:S(2)}, u32[]{:S(2)}) %all-to-all-start.3) | async-done | bytes 1441824 | tf_op jit(solution)/shard_map/all_to_all | solution.py:62
  212.7 0.9 pad_maximum_fusion
  (4 shorter events, 0.1 us)
Async XLA Ops:
  7.2 19.1 %copy-start.1 = (f32[3,88,1024]{2,1,0:T(8,128)S(1)}, f32[3,88,1024]{2,1,0:T(8,128)}, u32[]{:S(2)}) copy-start(f32[3,88,1024]{2,1,0:T(8,128)} %param.4) | copy-start | bytes 3244036
  8.1 45.1 %all-to-all-start = ((bf16[96,2,1408]{2,1,0:T(2,128)(2,1)}), bf16[96,2,1408]{2,1,0:T(2,128)(2,1)S(1)}, u32[]{:S(2)}, u32[]{:S(2)}) async-start(bf16[96,2,1408]{2,1,0:T(2,128)(2,1)} %reshape.51), calls=%async_computation | async-start | bytes 1081344 | tf_op jit(solution)/shard_map/all_to_all | solution.py:43
  54.7 8.1 %copy-start.2 = (s32[3]{0:T(128)S(1)}, s32[3]{0:T(128)}, u32[]{:S(2)}) copy-start(s32[3]{0:T(128)} %param.5) | copy-start | bytes 40
  56.3 49.2 %all-to-all-start.1 = ((f32[96,1,2816]{2,1,0:T(1,128)}), f32[96,1,2816]{2,1,0:T(1,128)S(1)}, u32[]{:S(2)}, u32[]{:S(2)}) async-start(f32[96,1,2816]{2,1,0:T(1,128)} %broadcast_in_dim.59), calls=%async_computation.1 | async-start | bytes 2162688 | tf_op jit(solution)/shard_map/all_to_all | solution.py:49
  108.5 18.8 %copy-start = (f32[3,88,1024]{2,1,0:T(8,128)}, f32[3,88,1024]{2,1,0:T(8,128)S(1)}, u32[]{:S(2)}) copy-start(f32[3,88,1024]{2,1,0:T(8,128)S(1)} %reshape.46) | copy-start | bytes 3244036
  176.6 36.1 %all-to-all-start.3 = ((bf16[8,88,1024]{2,1,0:T(8,128)(2,1)}), bf16[8,88,1024]{2,1,0:T(8,128)(2,1)S(1)}, u32[]{:S(2)}, u32[]{:S(2)}) async-start(bf16[8,88,1024]{2,1,0:T(8,128)(2,1)} %bitcast.7), calls=%async_computation.3 | async-start | bytes 2883584 | tf_op jit(solution)/shard_map/all_to_all | solution.py:62

commit v3 on v2

--- a/solution.py
+++ b/solution.py
@@ -47,8 +47,14 @@
     new_chunk = MOMENTUM_DECAY * momentum_chunk + summed_chunk
     spread = jnp.broadcast_to(new_chunk, (n_dp, chunk))
     new_momentum = lax.all_to_all(spread, "dp", 0, 0, tiled=True).reshape(momentum.shape)
-    partial_value = jnp.sum(new_momentum * new_momentum, axis=(1, 2))
-    squares = lax.psum(partial_value, "zero")
+    per_matrix = momentum[0].size
+    element = dp_index * chunk + lax.broadcasted_iota(jnp.int32, new_chunk.shape, 1)
+    which = element // per_matrix
+    squared_chunk = new_chunk * new_chunk
+    partial_value = jnp.stack(
+        [jnp.sum(jnp.where(which == j, squared_chunk, 0.0)) for j in range(momentum.shape[0])]
+    )
+    squares = lax.psum(partial_value, ("dp", "zero"))
     inverse = 1.0 / (jnp.sqrt(squares) + NORM_EPSILON)
     start_rows = (new_momentum * inverse[:, None, None]).astype(jnp.bfloat16)
     n_zero = lax.axis_size("zero")

time: 214 us -> 281 us (1.31)
  the two profiles are of different devices: /device:TPU:64 before, /device:TPU:1 now
where the time goes in v3:
time: 281 us; the launch traced here: 280 us
  blocking collectives  153 us (54%)
  waiting for transfers between devices  57.5 us (20%)
  starting transfers between devices  31.2 us (11%)
  other arithmetic  13.5 us (5%)
  matrix products  11.3 us (4%)
  local copies, waits for them, and re-layouts  7.42 us (3%)
  between operations  6.29 us (2%)
    psum x1, blocking collectives, on_device(): squares = lax.psum(partial_value, ('dp', 'zero'))  113 us
    all_to_all x1, blocking collectives, on_device(): incoming = lax.all_to_all(outgoing, 'zero', 0, 0, tiled=True)  39.7 us
    all_to_all x1, waiting for transfers between devices, on_device(): lax.all_to_all(result.reshape(incoming.shape), 'zero', 0, 0, tiled=True)  32.1 us
    all_to_all x1, waiting for transfers between devices, on_device(): lax.all_to_all(local_part.reshape(n_dp, chunk), 'dp', 0, 0, tiled=True)  25.4 us
    all_to_all x1, starting transfers between devices, on_device(): lax.all_to_all(local_part.reshape(n_dp, chunk), 'dp', 0, 0, tiled=True)  20 us
    all_to_all x1, starting transfers between devices, on_device(): lax.all_to_all(spread, 'dp', 0, 0, tiled=True).reshape(momentum.shape)  7.56 us
    dot_general x2, matrix products, orthogonalize(): jnp.dot(poly_term, current, preferred_element_type=jnp.float32)  6.58 us
  transfers between devices with their start and end apart: 3, of which 2 were waited for; matrix products, arithmetic and copies ran while one was open for 2% of the time, Pallas kernels for 0%

profile of v3, /device:TPU:1, one launch (start us, length us, event | category | flops | bytes accessed | tf_op | source)
XLA Modules:
  0.0 280.3 jit_solution(11349722397216371950)
XLA Ops:
  0.6 2.1 all_to_all.21
  2.8 0.5 broadcast.189
  3.3 3.9 %reduce.4 = bf16[96,2816]{1,0:T(8,128)(2,1)S(1)} reduce(bf16[96,1,2816]{2,1,0:T(2,128)(2,1)S(1)} %all_to_all.21, bf16[]{:T(256)} %broadcast.189), dimensions={1}, to_apply=%all_to_all.21.reduce_sub_computation | reduce | bytes 1081346 | tf_op jit(solution)/shard_map/all_to_all | solution.py:43
  7.2 0.0 copy-start.1
  7.2 0.9 reshape.103
  8.1 20.0 %all-to-all-start = ((bf16[96,2,1408]{2,1,0:T(2,128)(2,1)}), bf16[96,2,1408]{2,1,0:T(2,128)(2,1)S(1)}, u32[]{:S(2)}, u32[]{:S(2)}) async-start(bf16[96,2,1408]{2,1,0:T(2,128)(2,1)} %reshape.103), calls=%async_computation | async-start | bytes 1081344 | tf_op jit(solution)/shard_map/all_to_all | solution.py:43
  28.1 0.0 copy-done.1
  28.2 0.4 reshape.97
  28.5 25.4 %all-to-all-done = bf16[96,2,1408]{2,1,0:T(2,128)(2,1)S(1)} async-done(((bf16[96,2,1408]{2,1,0:T(2,128)(2,1)}), bf16[96,2,1408]{2,1,0:T(2,128)(2,1)S(1)}, u32[]{:S(2)}, u32[]{:S(2)}) %all-to-all-start) | async-done | bytes 540704 | tf_op jit(solution)/shard_map/all_to_all | solution.py:43
  54.0 0.4 reshape.104
  54.4 1.0 convert_reduce_fusion
  55.5 0.8 fusion
  56.3 0.0 copy-start.2
  56.3 1.5 broadcast_in_dim.65
  57.8 7.6 %all-to-all-start.1 = ((f32[96,1,2816]{2,1,0:T(1,128)}), f32[96,1,2816]{2,1,0:T(1,128)S(1)}, u32[]{:S(2)}, u32[]{:S(2)}) async-start(f32[96,1,2816]{2,1,0:T(1,128)} %broadcast_in_dim.65), calls=%async_computation.1 | async-start | bytes 2162688 | tf_op jit(solution)/shard_map/all_to_all | solution.py:49
  65.4 0.0 copy-done.2
  65.4 0.7 fusion.7
  66.0 1.3 iota_compare_fusion
  67.3 2.1 pad_maximum_fusion.1
  69.4 0.6 iota_compare_fusion.2
  69.9 113.4 %psum.7 = f32[3]{0:T(128)S(1)} all-reduce(f32[3]{0:T(128)S(1)} %pad_maximum_fusion.1), channel_id=1, replica_groups=mesh['dp'=96,'zero'=8] {'dp','zero'}, use_global_device_ids=true, to_apply=%region_4.5 | all-reduce | flops 3 | bytes 24 | tf_op jit(solution)/shard_map/psum | solution.py:57
  183.4 0.0 all-to-all-done.1
  183.4 2.6 reduce.2
  186.0 0.3 reshape.98
  186.3 0.0 copy-start
  186.3 0.1 multiply_convert_fusion.1
  186.5 0.3 select_select_fusion
  186.8 0.5 copy-done
  187.3 39.7 %all_to_all.26 = bf16[8,88,1024]{2,1,0:T(8,128)(2,1)S(1)} all-to-all(bf16[8,88,1024]{2,1,0:T(8,128)(2,1)S(1)} %select_select_fusion), channel_id=1, replica_groups=mesh['dp'=96,'zero'=8] {'zero'}, dimensions={0} | all-to-all | bytes 2883584 | tf_op jit(solution)/shard_map/all_to_all | solution.py:65
  227.0 1.3 convolution_convert_fusion.1
  228.3 3.3 %add_convert_fusion = bf16[704,1024]{1,0:T(8,128)(2,1)} fusion(bf16[704,1024]{1,0:T(8,128)(2,1)S(1)} %bitcast.28, bf16[704,704]{1,0:T(8,128)(2,1)S(1)} %convolution_convert_fusion.1), kind=kOutput, calls=%fused_computation.1 | convolution fusion | flops 1718210560 | bytes 3874816 | tf_op jit(solution)/shard_map/dot_general | solution.py:30
  231.6 0.0 copy-start.3
  231.6 3.4 %convolution_convert_fusion = bf16[704,704]{1,0:T(8,128)(2,1)S(1)} fusion(bf16[704,1024]{1,0:T(8,128)(2,1)} %add_convert_fusion), kind=kOutput, calls=%fused_computation.4 | convolution fusion | flops 1015517184 | bytes 2433024 | tf_op jit(solution)/shard_map/dot_general | solution.py:23
  235.0 0.0 copy-done.3
  235.0 3.3 %multiply_convert_fusion = bf16[704,1024]{1,0:T(8,128)(2,1)} fusion(bf16[704,1024]{1,0:T(8,128)(2,1)S(1)} %copy-done.3, bf16[704,704]{1,0:T(8,128)(2,1)S(1)} %convolution_convert_fusion), kind=kOutput, calls=%fused_computation | convolution fusion | flops 1718931456 | bytes 3874816 | tf_op jit(solution)/shard_map/dot_general | solution.py:30
  238.3 3.6 %all-to-all-start.3 = ((bf16[8,88,1024]{2,1,0:T(8,128)(2,1)}), bf16[8,88,1024]{2,1,0:T(8,128)(2,1)S(1)}, u32[]{:S(2)}, u32[]{:S(2)}) async-start(bf16[8,88,1024]{2,1,0:T(8,128)(2,1)} %bitcast.10), calls=%async_computation.3 | async-start | bytes 2883584 | tf_op jit(solution)/shard_map/all_to_all | solution.py:68
  247.3 32.1 %all-to-all-done.3 = bf16[8,88,1024]{2,1,0:T(8,128)(2,1)S(1)} async-done(((bf16[8,88,1024]{2,1,0:T(8,128)(2,1)}), bf16[8,88,1024]{2,1,0:T(8,128)(2,1)S(1)}, u32[]{:S(2)}, u32[]{:S(2)}) %all-to-all-start.3) | async-done | bytes 1441824 | tf_op jit(solution)/shard_map/all_to_all | solution.py:68
  279.4 0.9 pad_maximum_fusion
  (3 shorter events, 0.1 us)
Async XLA Ops:
  7.2 21.0 %copy-start.1 = (f32[3,88,1024]{2,1,0:T(8,128)S(1)}, f32[3,88,1024]{2,1,0:T(8,128)}, u32[]{:S(2)}) copy-start(f32[3,88,1024]{2,1,0:T(8,128)} %param.4) | copy-start | bytes 3244036
  8.1 45.9 %all-to-all-start = ((bf16[96,2,1408]{2,1,0:T(2,128)(2,1)}), bf16[96,2,1408]{2,1,0:T(2,128)(2,1)S(1)}, u32[]{:S(2)}, u32[]{:S(2)}) async-start(bf16[96,2,1408]{2,1,0:T(2,128)(2,1)} %reshape.103), calls=%async_computation | async-start | bytes 1081344 | tf_op jit(solution)/shard_map/all_to_all | solution.py:43
  56.3 9.1 %copy-start.2 = (s32[3]{0:T(128)S(1)}, s32[3]{0:T(128)}, u32[]{:S(2)}) copy-start(s32[3]{0:T(128)} %param.5) | copy-start | bytes 40
  57.8 125.6 %all-to-all-start.1 = ((f32[96,1,2816]{2,1,0:T(1,128)}), f32[96,1,2816]{2,1,0:T(1,128)S(1)}, u32[]{:S(2)}, u32[]{:S(2)}) async-start(f32[96,1,2816]{2,1,0:T(1,128)} %broadcast_in_dim.65), calls=%async_computation.1 | async-start | bytes 2162688 | tf_op jit(solution)/shard_map/all_to_all | solution.py:49
  186.3 1.0 copy-start
  231.6 3.4 %copy-start.3 = (bf16[704,1024]{1,0:T(8,128)(2,1)S(1)}, bf16[704,1024]{1,0:T(8,128)(2,1)}, u32[]{:S(2)}) copy-start(bf16[704,1024]{1,0:T(8,128)(2,1)} %add_convert_fusion) | copy-start | bytes 4325380
  238.3 41.1 %all-to-all-start.3 = ((bf16[8,88,1024]{2,1,0:T(8,128)(2,1)}), bf16[8,88,1024]{2,1,0:T(8,128)(2,1)S(1)}, u32[]{:S(2)}, u32[]{:S(2)}) async-start(bf16[8,88,1024]{2,1,0:T(8,128)(2,1)} %bitcast.10), calls=%async_computation.3 | async-start | bytes 2883584 | tf_op jit(solution)/shard_map/all_to_all | solution.py:68

commit v4 on v2

--- a/solution.py
+++ b/solution.py
@@ -52,14 +52,27 @@
     inverse = 1.0 / (jnp.sqrt(squares) + NORM_EPSILON)
     start_rows = (new_momentum * inverse[:, None, None]).astype(jnp.bfloat16)
     n_zero = lax.axis_size("zero")
+    core = dp_index % 2
+    siblings = [(d, d ^ 1) for d in range(n_dp)]
+    width = start_rows.shape[-1] // 2
+
+    def own_half(blocks):
+        return lax.dynamic_slice_in_dim(blocks, core * width, width, axis=2)
+
+    def both_halves(mine):
+        other = lax.ppermute(mine, "dp", siblings)
+        return jnp.where(core == 0, jnp.concatenate([mine, other], axis=2),
+                         jnp.concatenate([other, mine], axis=2))
+
     outgoing = jnp.zeros((n_zero,) + start_rows.shape[1:], start_rows.dtype)
     owners = jnp.arange(n_zero, dtype=owner_table.dtype)[:, None, None]
     for j in range(start_rows.shape[0]):
         outgoing = jnp.where(owners == owner_table[j], start_rows[j][None], outgoing)
-    incoming = lax.all_to_all(outgoing, "zero", 0, 0, tiled=True)
+    incoming = both_halves(lax.all_to_all(own_half(outgoing), "zero", 0, 0, tiled=True))
     full_matrix = incoming.reshape(-1, incoming.shape[-1])
     result = orthogonalize(full_matrix)
-    returned = lax.all_to_all(result.reshape(incoming.shape), "zero", 0, 0, tiled=True)
+    back = lax.all_to_all(own_half(result.reshape(incoming.shape)), "zero", 0, 0, tiled=True)
+    returned = both_halves(back)
     update_rows = jnp.stack(
         [lax.dynamic_index_in_dim(returned, owner_table[j], 0, keepdims=False)
          for j in range(start_rows.shape[0])]

time: 214 us -> 203 us (0.949)
  the two profiles are of different devices: /device:TPU:64 before, /device:TPU:1 now
where the time goes in v4:
time: 203 us; the launch traced here: 202 us
  waiting for transfers between devices  66.5 us (33%)
  blocking collectives  56.6 us (28%)
  starting transfers between devices  40.4 us (20%)
  matrix products  12.1 us (6%)
  other arithmetic  11.4 us (6%)
  local copies, waits for them, and re-layouts  8.2 us (4%)
  between operations  6.6 us (3%)
    all_to_all x1, waiting for transfers between devices, on_device(): lax.all_to_all(spread, 'dp', 0, 0, tiled=True).reshape(momentum.shape)  39.2 us
    all_to_all x1, waiting for transfers between devices, on_device(): lax.all_to_all(local_part.reshape(n_dp, chunk), 'dp', 0, 0, tiled=True)  25.4 us
    all_to_all x1, blocking collectives, on_device(): lax.all_to_all(own_half(result.reshape(incoming.shape)), 'zero', 0, 0, ti...  24.5 us
    all_to_all x1, starting transfers between devices, on_device(): lax.all_to_all(local_part.reshape(n_dp, chunk), 'dp', 0, 0, tiled=True)  20 us
    all_to_all x1, blocking collectives, on_device(): lax.all_to_all(own_half(outgoing), 'zero', 0, 0, tiled=True)  18 us
    psum x1, blocking collectives, on_device(): squares = lax.psum(partial_value, 'zero')  14.1 us
    ppermute x2, starting transfers between devices, both_halves(): other = lax.ppermute(mine, 'dp', siblings)  12.9 us
    dot_general x2, matrix products, orthogonalize(): jnp.dot(poly_term, current, preferred_element_type=jnp.float32)  8.53 us
  transfers between devices with their start and end apart: 4, of which 3 were waited for; matrix products, arithmetic and copies ran while one was open for 1% of the time, Pallas kernels for 0%

profile of v4, /device:TPU:1, one launch (start us, length us, event | category | flops | bytes accessed | tf_op | source)
XLA Modules:
  0.0 201.9 jit_solution(12754216515143058714)
XLA Ops:
  0.6 2.1 %all_to_all.21 = bf16[96,1,2816]{2,1,0:T(2,128)(2,1)S(1)} reshape(bf16[1,3,88,1024]{3,2,1,0:T(8,128)(2,1)} %param.3) | data formatting | bytes 1081344 | tf_op jit(solution)/shard_map/all_to_all | solution.py:43
  2.8 0.5 broadcast.60
  3.3 3.9 %reduce.4 = bf16[96,2816]{1,0:T(8,128)(2,1)S(1)} reduce(bf16[96,1,2816]{2,1,0:T(2,128)(2,1)S(1)} %all_to_all.21, bf16[]{:T(256)} %broadcast.60), dimensions={1}, to_apply=%all_to_all.21.reduce_sub_computation | reduce | bytes 1081346 | tf_op jit(solution)/shard_map/all_to_all | solution.py:43
  7.2 0.0 copy-start.1
  7.2 0.9 reshape.52
  8.1 20.0 %all-to-all-start = ((bf16[96,2,1408]{2,1,0:T(2,128)(2,1)}), bf16[96,2,1408]{2,1,0:T(2,128)(2,1)S(1)}, u32[]{:S(2)}, u32[]{:S(2)}) async-start(bf16[96,2,1408]{2,1,0:T(2,128)(2,1)} %reshape.52), calls=%async_computation | async-start | bytes 1081344 | tf_op jit(solution)/shard_map/all_to_all | solution.py:43
  28.1 0.0 copy-done.1
  28.2 0.4 reshape.47
  28.5 25.4 %all-to-all-done = bf16[96,2,1408]{2,1,0:T(2,128)(2,1)S(1)} async-done(((bf16[96,2,1408]{2,1,0:T(2,128)(2,1)}), bf16[96,2,1408]{2,1,0:T(2,128)(2,1)S(1)}, u32[]{:S(2)}, u32[]{:S(2)}) %all-to-all-start) | async-done | bytes 540704 | tf_op jit(solution)/shard_map/all_to_all | solution.py:43
  54.0 0.4 reshape.53
  54.4 1.0 convert_reduce_fusion
  55.5 0.0 copy-start.3
  55.5 1.5 broadcast_in_dim.59
  57.1 7.6 %all-to-all-start.1 = ((f32[96,1,2816]{2,1,0:T(1,128)}), f32[96,1,2816]{2,1,0:T(1,128)S(1)}, u32[]{:S(2)}, u32[]{:S(2)}) async-start(f32[96,1,2816]{2,1,0:T(1,128)} %broadcast_in_dim.59), calls=%async_computation.1 | async-start | bytes 2162688 | tf_op jit(solution)/shard_map/all_to_all | solution.py:49
  64.7 0.0 copy-done.3
  64.7 0.7 fusion.6
  65.3 0.7 iota_compare_fusion.2
  66.0 1.2 iota_compare_fusion
  67.3 39.2 %all-to-all-done.1 = f32[96,1,2816]{2,1,0:T(1,128)S(1)} async-done(((f32[96,1,2816]{2,1,0:T(1,128)}), f32[96,1,2816]{2,1,0:T(1,128)S(1)}, u32[]{:S(2)}, u32[]{:S(2)}) %all-to-all-start.1) | async-done | bytes 1081376 | tf_op jit(solution)/shard_map/all_to_all | solution.py:49
  106.5 2.6 %reduce.2 = f32[96,2816]{1,0:T(8,128)S(1)} reduce(f32[96,1,2816]{2,1,0:T(1,128)S(1)} %all-to-all-done.1, f32[]{:T(128)} %constant.53), dimensions={1}, to_apply=%all_to_all.18.reduce_sub_computation | reduce | bytes 2162692 | tf_op jit(solution)/shard_map/all_to_all | solution.py:49
  109.1 0.3 reshape.48
  109.4 0.0 copy-start
  109.4 0.2 multiply_reduce_fusion
  109.7 14.1 %psum.7 = f32[3]{0:T(128)S(1)} all-reduce(f32[3]{0:T(128)S(1)} %multiply_reduce_fusion), channel_id=1, replica_groups=mesh['dp'=96,'zero'=8] {'zero'}, use_global_device_ids=true, to_apply=%region_2.0 | all-reduce | flops 3 | bytes 24 | tf_op jit(solution)/shard_map/psum | solution.py:51
  123.7 0.2 multiply_convert_fusion.1
  124.0 0.0 copy-done
  124.0 0.3 select_select_fusion
  124.3 18.0 %all_to_all.26 = bf16[8,88,512]{2,1,0:T(8,128)(2,1)S(1)} all-to-all(bf16[8,88,512]{2,1,0:T(8,128)(2,1)S(1)} %select_select_fusion), channel_id=1, replica_groups=mesh['dp'=96,'zero'=8] {'zero'}, dimensions={0} | all-to-all | bytes 1441792 | tf_op jit(solution)/shard_map/all_to_all | solution.py:71
  142.3 10.4 %collective-permute-start = (bf16[8,88,512]{2,1,0:T(8,128)(2,1)S(1)}, bf16[8,88,512]{2,1,0:T(8,128)(2,1)S(1)}, u32[]{:S(2)}, u32[]{:S(2)}) collective-permute-start(bf16[8,88,512]{2,1,0:T(8,128)(2,1)S(1)} %all_to_all.26), channel_id=1, source_target_pairs={{0,8},{8,0},{16,24},{24,16},{32,40},{40,32},{48,56},{56,48},{64,72... | collective-permute-start | bytes 2162696 | tf_op jit(solution)/shard_map/ppermute | solution.py:63
  152.8 1.8 collective-permute-done
  154.6 2.3 %convolution_convert_fusion.1 = bf16[704,704]{1,0:T(8,128)(2,1)} fusion(bf16[704,512]{1,0:T(8,128)(2,1)S(1)} %bitcast.26, bf16[704,512]{1,0:T(8,128)(2,1)S(1)} %bitcast.22, pred[]{:T(512)S(6)} %eq.39), kind=kOutput, calls=%fused_computation.5 | convolution fusion | flops 1022005248 | bytes 2433025 | tf_op jit(solution)/shard_map/dot_general | solution.py:23
  156.9 4.4 %add_convert_fusion = bf16[704,1024]{1,0:T(8,128)(2,1)S(1)} fusion(bf16[704,704]{1,0:T(8,128)(2,1)} %convolution_convert_fusion.1, bf16[704,512]{1,0:T(8,128)(2,1)S(1)} %bitcast.23, bf16[704,512]{1,0:T(8,128)(2,1)S(1)} %bitcast.27, pred[]{:T(512)S(6)} %eq.39), kind=kOutput, calls=%fused_computation.1 | convolution fusion | flops 1731186688 | bytes 3874817 | tf_op jit(solution)/shard_map/dot_general | solution.py:30
  161.3 0.0 copy-start.4
  161.3 1.1 copy-done.4
  162.4 1.3 convolution_convert_fusion
  163.7 4.1 %multiply_convert_fusion = bf16[704,1024]{1,0:T(8,128)(2,1)S(1)} fusion(bf16[704,1024]{1,0:T(8,128)(2,1)} %copy-done.4, bf16[704,704]{1,0:T(8,128)(2,1)S(1)} %convolution_convert_fusion), kind=kOutput, calls=%fused_computation | convolution fusion | flops 1718931456 | bytes 3874816 | tf_op jit(solution)/shard_map/dot_general | solution.py:30
  167.8 0.0 copy-start.2
  167.8 0.1 constant_dynamic-slice_fusion.5
  167.9 24.5 %all_to_all.27 = bf16[8,88,512]{2,1,0:T(8,128)(2,1)S(1)} all-to-all(bf16[8,88,512]{2,1,0:T(8,128)(2,1)S(1)} %constant_dynamic-slice_fusion.5), channel_id=1, replica_groups=mesh['dp'=96,'zero'=8] {'zero'}, dimensions={0} | all-to-all | bytes 1441792 | tf_op jit(solution)/shard_map/all_to_all | solution.py:74
  192.5 0.0 copy-done.2
  192.5 2.4 %collective-permute-start.1 = (bf16[8,88,512]{2,1,0:T(8,128)(2,1)S(1)}, bf16[8,88,512]{2,1,0:T(8,128)(2,1)S(1)}, u32[]{:S(2)}, u32[]{:S(2)}) collective-permute-start(bf16[8,88,512]{2,1,0:T(8,128)(2,1)S(1)} %all_to_all.27), channel_id=1, source_target_pairs={{0,8},{8,0},{16,24},{24,16},{32,40},{40,32},{48,56},{56,48},{64,72... | collective-permute-start | bytes 2162696 | tf_op jit(solution)/shard_map/ppermute | solution.py:63
  200.6 0.0 collective-permute-done.1
  200.6 0.4 maximum_select_fusion.1
  201.1 0.9 pad_maximum_fusion
  (6 shorter events, 0.2 us)
Async XLA Ops:
  7.2 21.0 %copy-start.1 = (f32[3,88,1024]{2,1,0:T(8,128)S(1)}, f32[3,88,1024]{2,1,0:T(8,128)}, u32[]{:S(2)}) copy-start(f32[3,88,1024]{2,1,0:T(8,128)} %param.4) | copy-start | bytes 3244036
  8.1 45.9 %all-to-all-start = ((bf16[96,2,1408]{2,1,0:T(2,128)(2,1)}), bf16[96,2,1408]{2,1,0:T(2,128)(2,1)S(1)}, u32[]{:S(2)}, u32[]{:S(2)}) async-start(bf16[96,2,1408]{2,1,0:T(2,128)(2,1)} %reshape.52), calls=%async_computation | async-start | bytes 1081344 | tf_op jit(solution)/shard_map/all_to_all | solution.py:43
  55.5 9.1 %copy-start.3 = (s32[3]{0:T(128)S(1)}, s32[3]{0:T(128)}, u32[]{:S(2)}) copy-start(s32[3]{0:T(128)} %param.5) | copy-start | bytes 40
  57.1 49.4 %all-to-all-start.1 = ((f32[96,1,2816]{2,1,0:T(1,128)}), f32[96,1,2816]{2,1,0:T(1,128)S(1)}, u32[]{:S(2)}, u32[]{:S(2)}) async-start(f32[96,1,2816]{2,1,0:T(1,128)} %broadcast_in_dim.59), calls=%async_computation.1 | async-start | bytes 2162688 | tf_op jit(solution)/shard_map/all_to_all | solution.py:49
  109.4 14.5 %copy-start = (f32[3,88,1024]{2,1,0:T(8,128)}, f32[3,88,1024]{2,1,0:T(8,128)S(1)}, u32[]{:S(2)}) copy-start(f32[3,88,1024]{2,1,0:T(8,128)S(1)} %reshape.48) | copy-start | bytes 3244036
  142.3 12.2 %collective-permute-start = (bf16[8,88,512]{2,1,0:T(8,128)(2,1)S(1)}, bf16[8,88,512]{2,1,0:T(8,128)(2,1)S(1)}, u32[]{:S(2)}, u32[]{:S(2)}) collective-permute-start(bf16[8,88,512]{2,1,0:T(8,128)(2,1)S(1)} %all_to_all.26), channel_id=1, source_target_pairs={{0,8},{8,0},{16,24},{24,16},{32,40},{40,32},{48,56},{56,48},{64,72... | collective-permute-start | bytes 2162696 | tf_op jit(solution)/shard_map/ppermute | solution.py:63
  161.3 1.1 copy-start.4
  167.8 24.6 %copy-start.2 = (bf16[704,1024]{1,0:T(8,128)(2,1)}, bf16[704,1024]{1,0:T(8,128)(2,1)S(1)}, u32[]{:S(2)}) copy-start(bf16[704,1024]{1,0:T(8,128)(2,1)S(1)} %multiply_convert_fusion) | copy-start | bytes 4325380
  192.5 8.1 %collective-permute-start.1 = (bf16[8,88,512]{2,1,0:T(8,128)(2,1)S(1)}, bf16[8,88,512]{2,1,0:T(8,128)(2,1)S(1)}, u32[]{:S(2)}, u32[]{:S(2)}) collective-permute-start(bf16[8,88,512]{2,1,0:T(8,128)(2,1)S(1)} %all_to_all.27), channel_id=1, source_target_pairs={{0,8},{8,0},{16,24},{24,16},{32,40},{40,32},{48,56},{56,48},{64,72... | collective-permute-start | bytes 2162696 | tf_op jit(solution)/shard_map/ppermute | solution.py:63

commit v5 on v4

--- a/solution.py
+++ b/solution.py
@@ -3,7 +3,7 @@
 import jax
 import jax.numpy as jnp
 from jax import lax
-from jax.sharding import PartitionSpec as P
+from jax.sharding import Mesh, PartitionSpec as P
 
 D = 1024
 ITERS = 2
@@ -14,6 +14,7 @@
 COEF_C = 2.0315
 MOMENTUM_DECAY = 0.95
 NORM_EPSILON = 1e-07
+DP = ("chip", "core")
 
 
 def orthogonalize(matrix):
@@ -37,30 +38,33 @@
 
 def on_device(grad_parts, momentum, owner_table):
     my_index = lax.axis_index("zero")
-    n_dp = lax.axis_size("dp")
+    n_chip = lax.axis_size("chip")
+    n_dp = n_chip * lax.axis_size("core")
+    core = lax.axis_index("core")
     local_part = grad_parts[0]
     chunk = local_part.size // n_dp
-    pieces = lax.all_to_all(local_part.reshape(n_dp, chunk), "dp", 0, 0, tiled=True)
+    pieces = lax.all_to_all(local_part.reshape(n_dp, chunk), DP, 0, 0, tiled=True)
     summed_chunk = jnp.sum(pieces.astype(jnp.float32), axis=0, keepdims=True)
-    dp_index = lax.axis_index("dp")
+    dp_index = lax.axis_index("chip") * 2 + core
     momentum_chunk = lax.dynamic_slice_in_dim(momentum.reshape(n_dp, chunk), dp_index, 1, 0)
     new_chunk = MOMENTUM_DECAY * momentum_chunk + summed_chunk
-    spread = jnp.broadcast_to(new_chunk, (n_dp, chunk))
-    new_momentum = lax.all_to_all(spread, "dp", 0, 0, tiled=True).reshape(momentum.shape)
+    spread = jnp.broadcast_to(new_chunk, (n_chip, chunk))
+    mine = lax.all_to_all(spread, "chip", 0, 0, tiled=True)
+    other = lax.ppermute(mine, "core", [(0, 1), (1, 0)])
+    ordered = jnp.where(core == 0, jnp.stack([mine, other], axis=1), jnp.stack([other, mine], axis=1))
+    new_momentum = ordered.reshape(momentum.shape)
     partial_value = jnp.sum(new_momentum * new_momentum, axis=(1, 2))
     squares = lax.psum(partial_value, "zero")
     inverse = 1.0 / (jnp.sqrt(squares) + NORM_EPSILON)
     start_rows = (new_momentum * inverse[:, None, None]).astype(jnp.bfloat16)
     n_zero = lax.axis_size("zero")
-    core = dp_index % 2
-    siblings = [(d, d ^ 1) for d in range(n_dp)]
     width = start_rows.shape[-1] // 2
 
     def own_half(blocks):
         return lax.dynamic_slice_in_dim(blocks, core * width, width, axis=2)
 
     def both_halves(mine):
-        other = lax.ppermute(mine, "dp", siblings)
+        other = lax.ppermute(mine, "core", [(0, 1), (1, 0)])
         return jnp.where(core == 0, jnp.concatenate([mine, other], axis=2),
                          jnp.concatenate([other, mine], axis=2))
 
@@ -81,10 +85,12 @@
 
 
 def solution(mesh):
-    placed = (P("dp", None, "zero", None), P(None, "zero", None), P())
+    n_dp, n_zero = mesh.devices.shape
+    split = Mesh(mesh.devices.reshape(n_dp // 2, 2, n_zero), ("chip", "core", "zero"))
+    placed = (P(DP, None, "zero", None), P(None, "zero", None), P())
     return jax.shard_map(
         on_device,
-        mesh=mesh,
+        mesh=split,
         in_specs=placed,
         out_specs=(P(None, "zero", None), P(None, "zero", None), P("zero", None, None)),
         check_vma=False,

time: 203 us -> 187 us (0.921)
  waiting for transfers between devices: 66.5 us -> 27.2 us
  blocking collectives: 56.6 us -> 88.3 us
  starting transfers between devices: 40.4 us -> 34.4 us
    all_to_all x2 -> x1, waiting for transfers between devices: 64.7 us -> 25.4 us  [on_device(): lax.all_to_all(local_part.reshape(n_dp, chunk), DP, 0, 0, tiled=True)]
    all_to_all x0 -> x1, blocking collectives: none -> 28.3 us  [on_device(): mine = lax.all_to_all(spread, 'chip', 0, 0, tiled=True)]
    all_to_all x2 -> x1, starting transfers between devices: 27.6 us -> 20 us  [on_device(): lax.all_to_all(local_part.reshape(n_dp, chunk), DP, 0, 0, tiled=True)]
    all_to_all x1, blocking collectives: 18 us -> 21.4 us  [on_device(): lax.all_to_all(own_half(outgoing), 'zero', 0, 0, tiled=True)]
    all_to_all x2 -> x1, other arithmetic: 6.54 us -> 3.89 us  [on_device(): lax.all_to_all(local_part.reshape(n_dp, chunk), DP, 0, 0, tiled=True)]
    ppermute x2 -> x3, starting transfers between devices: 12.9 us -> 14.4 us  [the longest x2 9.64 us: both_halves(): other = lax.ppermute(mine, 'core', [(0, 1), (1, 0)])]
  transfers between devices with their start and end apart: 4 -> 4, of which waited for: 3 -> 2; matrix products, arithmetic and copies ran while one was open for 1% -> 2% of each run, Pallas kernels for 0% -> 0%
where the time goes in v5:
time: 187 us
  blocking collectives  88.3 us (47%)
  starting transfers between devices  34.4 us (18%)
  waiting for transfers between devices  27.2 us (15%)
  matrix products  12.2 us (7%)
  other arithmetic  10.3 us (6%)
  local copies, waits for them, and re-layouts  7.87 us (4%)
  between operations  6.46 us (3%)
    all_to_all x1, blocking collectives, on_device(): mine = lax.all_to_all(spread, 'chip', 0, 0, tiled=True)  28.3 us
    all_to_all x1, waiting for transfers between devices, on_device(): lax.all_to_all(local_part.reshape(n_dp, chunk), DP, 0, 0, tiled=True)  25.4 us
    all_to_all x1, blocking collectives, on_device(): lax.all_to_all(own_half(result.reshape(incoming.shape)), 'zero', 0, 0, ti...  24.6 us
    all_to_all x1, blocking collectives, on_device(): lax.all_to_all(own_half(outgoing), 'zero', 0, 0, tiled=True)  21.4 us
    all_to_all x1, starting transfers between devices, on_device(): lax.all_to_all(local_part.reshape(n_dp, chunk), DP, 0, 0, tiled=True)  20 us
    psum x1, blocking collectives, on_device(): squares = lax.psum(partial_value, 'zero')  14 us
    ppermute x2, starting transfers between devices, both_halves(): other = lax.ppermute(mine, 'core', [(0, 1), (1, 0)])  9.64 us
    dot_general x2, matrix products, orthogonalize(): jnp.dot(poly_term, current, preferred_element_type=jnp.float32)  8.53 us
  transfers between devices with their start and end apart: 4, of which 2 were waited for; matrix products, arithmetic and copies ran while one was open for 2% of the time, Pallas kernels for 0%

profile of v5, /device:TPU:1, one launch (start us, length us, event | category | flops | bytes accessed | tf_op | source)
XLA Modules:
  0.0 186.7 jit_solution(1566852646893743192)
XLA Ops:
  0.6 2.1 %all_to_all.24 = bf16[96,1,2816]{2,1,0:T(2,128)(2,1)S(1)} reshape(bf16[1,3,88,1024]{3,2,1,0:T(8,128)(2,1)} %param.3) | data formatting | bytes 1081344 | tf_op jit(solution)/shard_map/all_to_all | solution.py:46
  2.8 0.5 broadcast.61
  3.3 3.9 %reduce.3 = bf16[96,2816]{1,0:T(8,128)(2,1)S(1)} reduce(bf16[96,1,2816]{2,1,0:T(2,128)(2,1)S(1)} %all_to_all.24, bf16[]{:T(256)} %broadcast.61), dimensions={1}, to_apply=%all_to_all.24.reduce_sub_computation | reduce | bytes 1081346 | tf_op jit(solution)/shard_map/all_to_all | solution.py:46
  7.2 0.0 copy-start.1
  7.2 0.9 reshape.52
  8.1 20.0 %all-to-all-start = ((bf16[96,2,1408]{2,1,0:T(2,128)(2,1)}), bf16[96,2,1408]{2,1,0:T(2,128)(2,1)S(1)}, u32[]{:S(2)}, u32[]{:S(2)}) async-start(bf16[96,2,1408]{2,1,0:T(2,128)(2,1)} %reshape.52), calls=%async_computation | async-start | bytes 1081344 | tf_op jit(solution)/shard_map/all_to_all | solution.py:46
  28.1 0.0 copy-done.1
  28.2 0.4 reshape.49
  28.5 25.4 %all-to-all-done = bf16[96,2,1408]{2,1,0:T(2,128)(2,1)S(1)} async-done(((bf16[96,2,1408]{2,1,0:T(2,128)(2,1)}), bf16[96,2,1408]{2,1,0:T(2,128)(2,1)S(1)}, u32[]{:S(2)}, u32[]{:S(2)}) %all-to-all-start) | async-done | bytes 540704 | tf_op jit(solution)/shard_map/all_to_all | solution.py:46
  54.0 0.4 reshape.53
  54.4 1.0 convert_reduce_fusion
  55.5 0.0 copy-start.3
  55.5 0.3 broadcast_in_dim.59
  55.8 28.3 %all_to_all.29 = f32[48,1,2816]{2,1,0:T(1,128)S(1)} all-to-all(f32[48,1,2816]{2,1,0:T(1,128)S(1)} %broadcast_in_dim.59), channel_id=1, replica_groups=mesh['chip'=48,'core'=2,'zero'=8] {'chip'}, dimensions={0} | all-to-all | bytes 1081344 | tf_op jit(solution)/shard_map/all_to_all | solution.py:52
  84.1 4.8 %collective-permute-start = (f32[48,2816]{1,0:T(8,128)S(1)}, f32[48,2816]{1,0:T(8,128)S(1)}, u32[]{:S(2)}, u32[]{:S(2)}) collective-permute-start(f32[48,2816]{1,0:T(8,128)S(1)} %bitcast.27), channel_id=1, source_target_pairs={{0,8},{8,0},{1,9},{9,1},{2,10},{10,2},{3,11},{11,3},{4,12},{12,4},... | collective-permute-start | bytes 1622024 | tf_op jit(solution)/shard_map/ppermute | solution.py:53
  88.9 0.0 copy-done.3
  88.9 0.6 fusion.6
  89.5 0.6 iota_compare_fusion.2
  90.1 1.3 iota_compare_fusion
  91.4 0.0 collective-permute-done
  91.4 0.4 stack.8
  91.8 1.5 maximum_select_fusion.2
  93.3 0.9 select_n.57
  94.2 0.0 copy-start
  94.2 0.2 multiply_reduce_fusion
  94.4 14.0 %psum.7 = f32[3]{0:T(128)S(1)} all-reduce(f32[3]{0:T(128)S(1)} %multiply_reduce_fusion), channel_id=1, replica_groups=mesh['chip'=48,'core'=2,'zero'=8] {'zero'}, use_global_device_ids=true, to_apply=%region_2.3 | all-reduce | flops 3 | bytes 24 | tf_op jit(solution)/shard_map/psum | solution.py:57
  108.5 0.2 multiply_convert_fusion.1
  108.7 0.0 copy-done
  108.7 0.3 select_select_fusion
  109.0 21.4 %all_to_all.30 = bf16[8,88,512]{2,1,0:T(8,128)(2,1)S(1)} all-to-all(bf16[8,88,512]{2,1,0:T(8,128)(2,1)S(1)} %select_select_fusion), channel_id=1, replica_groups=mesh['chip'=48,'core'=2,'zero'=8] {'zero'}, dimensions={0} | all-to-all | bytes 1441792 | tf_op jit(solution)/shard_map/all_to_all | solution.py:75
  130.4 7.2 %collective-permute-start.1 = (bf16[8,88,512]{2,1,0:T(8,128)(2,1)S(1)}, bf16[8,88,512]{2,1,0:T(8,128)(2,1)S(1)}, u32[]{:S(2)}, u32[]{:S(2)}) collective-permute-start(bf16[8,88,512]{2,1,0:T(8,128)(2,1)S(1)} %all_to_all.30), channel_id=1, source_target_pairs={{0,8},{8,0},{1,9},{9,1},{2,10},{10,2},{3,11},{11,3},{4,12},{12,4},... | collective-permute-start | bytes 2162696 | tf_op jit(solution)/shard_map/ppermute | solution.py:67
  137.7 1.8 collective-permute-done.1
  139.5 2.3 %convolution_convert_fusion.1 = bf16[704,704]{1,0:T(8,128)(2,1)} fusion(bf16[704,512]{1,0:T(8,128)(2,1)S(1)} %bitcast.30, bf16[704,512]{1,0:T(8,128)(2,1)S(1)} %bitcast.25, pred[]{:T(512)S(6)} %eq.38), kind=kOutput, calls=%fused_computation.5 | convolution fusion | flops 1022005248 | bytes 2433025 | tf_op jit(solution)/shard_map/dot_general | solution.py:24
  141.8 4.4 %add_convert_fusion = bf16[704,1024]{1,0:T(8,128)(2,1)S(1)} fusion(bf16[704,704]{1,0:T(8,128)(2,1)} %convolution_convert_fusion.1, bf16[704,512]{1,0:T(8,128)(2,1)S(1)} %bitcast.26, bf16[704,512]{1,0:T(8,128)(2,1)S(1)} %bitcast.31, pred[]{:T(512)S(6)} %eq.38), kind=kOutput, calls=%fused_computation.1 | convolution fusion | flops 1731186688 | bytes 3874817 | tf_op jit(solution)/shard_map/dot_general | solution.py:31
  146.2 0.0 copy-start.4
  146.2 1.1 copy-done.4
  147.3 1.3 convolution_convert_fusion
  148.6 4.1 %multiply_convert_fusion = bf16[704,1024]{1,0:T(8,128)(2,1)S(1)} fusion(bf16[704,1024]{1,0:T(8,128)(2,1)} %copy-done.4, bf16[704,704]{1,0:T(8,128)(2,1)S(1)} %convolution_convert_fusion), kind=kOutput, calls=%fused_computation | convolution fusion | flops 1718931456 | bytes 3874816 | tf_op jit(solution)/shard_map/dot_general | solution.py:31
  152.8 0.0 copy-start.2
  152.8 0.1 constant_dynamic-slice_fusion.5
  152.8 24.6 %all_to_all.31 = bf16[8,88,512]{2,1,0:T(8,128)(2,1)S(1)} all-to-all(bf16[8,88,512]{2,1,0:T(8,128)(2,1)S(1)} %constant_dynamic-slice_fusion.5), channel_id=1, replica_groups=mesh['chip'=48,'core'=2,'zero'=8] {'zero'}, dimensions={0} | all-to-all | bytes 1441792 | tf_op jit(solution)/shard_map/all_to_all | solution.py:78
  177.4 0.0 copy-done.2
  177.4 2.4 %collective-permute-start.2 = (bf16[8,88,512]{2,1,0:T(8,128)(2,1)S(1)}, bf16[8,88,512]{2,1,0:T(8,128)(2,1)S(1)}, u32[]{:S(2)}, u32[]{:S(2)}) collective-permute-start(bf16[8,88,512]{2,1,0:T(8,128)(2,1)S(1)} %all_to_all.31), channel_id=1, source_target_pairs={{0,8},{8,0},{1,9},{9,1},{2,10},{10,2},{3,11},{11,3},{4,12},{12,4},... | collective-permute-start | bytes 2162696 | tf_op jit(solution)/shard_map/ppermute | solution.py:67
  185.3 0.0 collective-permute-done.2
  185.3 0.4 maximum_select_fusion.1
  185.8 0.9 pad_maximum_fusion
  (7 shorter events, 0.2 us)
Async XLA Ops:
  7.2 21.0 %copy-start.1 = (f32[3,88,1024]{2,1,0:T(8,128)S(1)}, f32[3,88,1024]{2,1,0:T(8,128)}, u32[]{:S(2)}) copy-start(f32[3,88,1024]{2,1,0:T(8,128)} %param.4) | copy-start | bytes 3244036
  8.1 45.9 %all-to-all-start = ((bf16[96,2,1408]{2,1,0:T(2,128)(2,1)}), bf16[96,2,1408]{2,1,0:T(2,128)(2,1)S(1)}, u32[]{:S(2)}, u32[]{:S(2)}) async-start(bf16[96,2,1408]{2,1,0:T(2,128)(2,1)} %reshape.52), calls=%async_computation | async-start | bytes 1081344 | tf_op jit(solution)/shard_map/all_to_all | solution.py:46
  55.5 33.4 %copy-start.3 = (s32[3]{0:T(128)S(1)}, s32[3]{0:T(128)}, u32[]{:S(2)}) copy-start(s32[3]{0:T(128)} %param.5) | copy-start | bytes 40
  84.1 7.3 %collective-permute-start = (f32[48,2816]{1,0:T(8,128)S(1)}, f32[48,2816]{1,0:T(8,128)S(1)}, u32[]{:S(2)}, u32[]{:S(2)}) collective-permute-start(f32[48,2816]{1,0:T(8,128)S(1)} %bitcast.27), channel_id=1, source_target_pairs={{0,8},{8,0},{1,9},{9,1},{2,10},{10,2},{3,11},{11,3},{4,12},{12,4},... | collective-permute-start | bytes 1622024 | tf_op jit(solution)/shard_map/ppermute | solution.py:53
  94.2 14.5 %copy-start = (f32[3,88,1024]{2,1,0:T(8,128)}, f32[3,88,1024]{2,1,0:T(8,128)S(1)}, u32[]{:S(2)}) copy-start(f32[3,88,1024]{2,1,0:T(8,128)S(1)} %select_n.57) | copy-start | bytes 3244036
  130.4 9.0 %collective-permute-start.1 = (bf16[8,88,512]{2,1,0:T(8,128)(2,1)S(1)}, bf16[8,88,512]{2,1,0:T(8,128)(2,1)S(1)}, u32[]{:S(2)}, u32[]{:S(2)}) collective-permute-start(bf16[8,88,512]{2,1,0:T(8,128)(2,1)S(1)} %all_to_all.30), channel_id=1, source_target_pairs={{0,8},{8,0},{1,9},{9,1},{2,10},{10,2},{3,11},{11,3},{4,12},{12,4},... | collective-permute-start | bytes 2162696 | tf_op jit(solution)/shard_map/ppermute | solution.py:67
  146.2 1.1 copy-start.4
  152.8 24.7 %copy-start.2 = (bf16[704,1024]{1,0:T(8,128)(2,1)}, bf16[704,1024]{1,0:T(8,128)(2,1)S(1)}, u32[]{:S(2)}) copy-start(bf16[704,1024]{1,0:T(8,128)(2,1)S(1)} %multiply_convert_fusion) | copy-start | bytes 4325380
  177.4 7.9 %collective-permute-start.2 = (bf16[8,88,512]{2,1,0:T(8,128)(2,1)S(1)}, bf16[8,88,512]{2,1,0:T(8,128)(2,1)S(1)}, u32[]{:S(2)}, u32[]{:S(2)}) collective-permute-start(bf16[8,88,512]{2,1,0:T(8,128)(2,1)S(1)} %all_to_all.31), channel_id=1, source_target_pairs={{0,8},{8,0},{1,9},{9,1},{2,10},{10,2},{3,11},{11,3},{4,12},{12,4},... | collective-permute-start | bytes 2162696 | tf_op jit(solution)/shard_map/ppermute | solution.py:67

commit v6 on v5

--- a/solution.py
+++ b/solution.py
@@ -43,8 +43,12 @@
     core = lax.axis_index("core")
     local_part = grad_parts[0]
     chunk = local_part.size // n_dp
-    pieces = lax.all_to_all(local_part.reshape(n_dp, chunk), DP, 0, 0, tiled=True)
-    summed_chunk = jnp.sum(pieces.astype(jnp.float32), axis=0, keepdims=True)
+    by_core = local_part.reshape(n_chip, 2, chunk)
+    kept = lax.dynamic_index_in_dim(by_core, core, axis=1, keepdims=False)
+    given = lax.dynamic_index_in_dim(by_core, 1 - core, axis=1, keepdims=False)
+    taken = lax.ppermute(given, "core", [(0, 1), (1, 0)])
+    pieces = lax.all_to_all(jnp.stack([kept, taken], axis=1), "chip", 0, 0, tiled=True)
+    summed_chunk = jnp.sum(pieces.astype(jnp.float32), axis=(0, 1))[None]
     dp_index = lax.axis_index("chip") * 2 + core
     momentum_chunk = lax.dynamic_slice_in_dim(momentum.reshape(n_dp, chunk), dp_index, 1, 0)
     new_chunk = MOMENTUM_DECAY * momentum_chunk + summed_chunk

time: 187 us -> 187 us (level)
  blocking collectives: 88.3 us -> 91.7 us
  other arithmetic: 10.3 us -> 7.87 us
  waiting for transfers between devices: 27.2 us -> 25.2 us
    ppermute x0 -> x1, starting transfers between devices: none -> 12.4 us  [on_device(): taken = lax.ppermute(given, 'core', [(0, 1), (1, 0)])]
    all_to_all x1, starting transfers between devices: 20 us -> 9.03 us  [on_device(): lax.all_to_all(jnp.stack([kept, taken], axis=1), 'chip', 0, 0, tiled=True)]
    all_to_all x1 -> x0, other arithmetic: 3.89 us -> none  [on_device(): lax.all_to_all(local_part.reshape(n_dp, chunk), DP, 0, 0, tiled=True)]
    all_to_all x1, blocking collectives: 28.3 us -> 31.9 us  [on_device(): mine = lax.all_to_all(spread, 'chip', 0, 0, tiled=True)]
    all_to_all x1, waiting for transfers between devices: 25.4 us -> 22.4 us  [on_device(): lax.all_to_all(jnp.stack([kept, taken], axis=1), 'chip', 0, 0, tiled=True)]
    all_to_all x2 -> x0, local copies, waits for them, and re-layouts: 2.64 us -> none  [on_device(): lax.all_to_all(local_part.reshape(n_dp, chunk), DP, 0, 0, tiled=True)]
    another operation x0 -> x1, other arithmetic: none -> 2.03 us  [on_device(): jnp.stack([kept, taken], axis=1)]
  transfers between devices with their start and end apart: 4 -> 5, of which waited for: 2 -> 3; matrix products, arithmetic and copies ran while one was open for 2% -> 2% of each run, Pallas kernels for 0% -> 0%
where the time goes in v6:
time: 187 us
  blocking collectives  91.7 us (49%)
  starting transfers between devices  36.2 us (19%)
  waiting for transfers between devices  25.2 us (13%)
  matrix products  12.2 us (7%)
  other arithmetic  7.87 us (4%)
  local copies, waits for them, and re-layouts  6.88 us (4%)
  between operations  6.64 us (4%)
    all_to_all x1, blocking collectives, on_device(): mine = lax.all_to_all(spread, 'chip', 0, 0, tiled=True)  31.9 us
    all_to_all x1, blocking collectives, on_device(): lax.all_to_all(own_half(result.reshape(incoming.shape)), 'zero', 0, 0, ti...  24.6 us
    all_to_all x1, waiting for transfers between devices, on_device(): lax.all_to_all(jnp.stack([kept, taken], axis=1), 'chip', 0, 0, tiled=True)  22.4 us
    all_to_all x1, blocking collectives, on_device(): lax.all_to_all(own_half(outgoing), 'zero', 0, 0, tiled=True)  21.4 us
    psum x1, blocking collectives, on_device(): squares = lax.psum(partial_value, 'zero')  13.8 us
    ppermute x1, starting transfers between devices, on_device(): taken = lax.ppermute(given, 'core', [(0, 1), (1, 0)])  12.4 us
    ppermute x2, starting transfers between devices, both_halves(): other = lax.ppermute(mine, 'core', [(0, 1), (1, 0)])  9.82 us
    all_to_all x1, starting transfers between devices, on_device(): lax.all_to_all(jnp.stack([kept, taken], axis=1), 'chip', 0, 0, tiled=True)  9.03 us
  transfers between devices with their start and end apart: 5, of which 3 were waited for; matrix products, arithmetic and copies ran while one was open for 2% of the time, Pallas kernels for 0%

profile of v6, /device:TPU:1, one launch (start us, length us, event | category | flops | bytes accessed | tf_op | source)
XLA Modules:
  0.0 186.6 jit_solution(11953091403728595268)
XLA Ops:
  0.6 1.4 reshape_squeeze.3
  2.0 1.1 constant_dynamic-slice_fusion.8
  3.2 12.4 %collective-permute-start = (bf16[48,2816]{1,0:T(8,128)(2,1)S(1)}, bf16[48,2816]{1,0:T(8,128)(2,1)S(1)}, u32[]{:S(2)}, u32[]{:S(2)}) collective-permute-start(bf16[48,2816]{1,0:T(8,128)(2,1)S(1)} %bitcast.34), channel_id=1, source_target_pairs={{0,8},{8,0},{1,9},{9,1},{2,10},{10,2},{3,11},{11,3},{4,12},{12,4},... | collective-permute-start | bytes 811016 | tf_op jit(solution)/shard_map/ppermute | solution.py:49
  15.6 1.2 collective-permute-done
  16.7 0.4 copy.6
  17.2 0.0 copy-start.1
  17.2 2.0 %pad_maximum_fusion = bf16[48,2,2816]{2,1,0:T(2,128)(2,1)} fusion(bf16[48,1,2816]{2,1,0:T(2,128)(2,1)S(1)} %copy.6, bf16[48,1,2816]{2,1,0:T(2,128)(2,1)S(1)} %get-tuple-element.9), kind=kLoop, calls=%fused_computation.13 | loop fusion | flops 1081344 | bytes 1081344 | tf_op jit(solution)/shard_map/stack | solution.py:50
  19.2 9.0 %all-to-all-start = ((bf16[48,2,2816]{2,1,0:T(2,128)(2,1)}), bf16[48,2,2816]{2,1,0:T(2,128)(2,1)S(1)}, u32[]{:S(2)}, u32[]{:S(2)}) async-start(bf16[48,2,2816]{2,1,0:T(2,128)(2,1)} %pad_maximum_fusion), calls=%async_computation | async-start | bytes 1081344 | tf_op jit(solution)/shard_map/all_to_all | solution.py:50
  28.3 0.0 copy-done.1
  28.3 0.4 reshape.45
  28.7 22.4 %all-to-all-done = bf16[48,2,2816]{2,1,0:T(2,128)(2,1)S(1)} async-done(((bf16[48,2,2816]{2,1,0:T(2,128)(2,1)}), bf16[48,2,2816]{2,1,0:T(2,128)(2,1)S(1)}, u32[]{:S(2)}, u32[]{:S(2)}) %all-to-all-start) | async-done | bytes 540704 | tf_op jit(solution)/shard_map/all_to_all | solution.py:50
  51.1 0.4 convert_reduce_fusion
  51.5 0.0 copy-start.3
  51.5 0.1 add_reduce_fusion
  51.6 0.3 broadcast_in_dim.59
  51.9 31.9 %all_to_all.24 = f32[48,1,2816]{2,1,0:T(1,128)S(1)} all-to-all(f32[48,1,2816]{2,1,0:T(1,128)S(1)} %broadcast_in_dim.59), channel_id=1, replica_groups=mesh['chip'=48,'core'=2,'zero'=8] {'chip'}, dimensions={0} | all-to-all | bytes 1081344 | tf_op jit(solution)/shard_map/all_to_all | solution.py:56
  83.8 5.0 %collective-permute-start.1 = (f32[48,2816]{1,0:T(8,128)S(1)}, f32[48,2816]{1,0:T(8,128)S(1)}, u32[]{:S(2)}, u32[]{:S(2)}) collective-permute-start(f32[48,2816]{1,0:T(8,128)S(1)} %bitcast.31), channel_id=1, source_target_pairs={{0,8},{8,0},{1,9},{9,1},{2,10},{10,2},{3,11},{11,3},{4,12},{12,4},... | collective-permute-start | bytes 1622024 | tf_op jit(solution)/shard_map/ppermute | solution.py:57
  88.8 0.0 copy-done.3
  88.8 0.7 fusion.6
  89.5 0.6 iota_compare_fusion.2
  90.0 1.3 iota_compare_fusion
  91.4 0.0 collective-permute-done.1
  91.4 0.4 stack.27
  91.8 1.5 maximum_select_fusion.2
  93.3 0.9 select_n.66
  94.2 0.0 copy-start
  94.2 0.2 multiply_reduce_fusion
  94.4 13.8 %psum.7 = f32[3]{0:T(128)S(1)} all-reduce(f32[3]{0:T(128)S(1)} %multiply_reduce_fusion), channel_id=1, replica_groups=mesh['chip'=48,'core'=2,'zero'=8] {'zero'}, use_global_device_ids=true, to_apply=%region_2.3 | all-reduce | flops 3 | bytes 24 | tf_op jit(solution)/shard_map/psum | solution.py:61
  108.3 0.2 multiply_convert_fusion.1
  108.5 0.0 copy-done
  108.5 0.3 select_select_fusion
  108.8 21.4 %all_to_all.25 = bf16[8,88,512]{2,1,0:T(8,128)(2,1)S(1)} all-to-all(bf16[8,88,512]{2,1,0:T(8,128)(2,1)S(1)} %select_select_fusion), channel_id=1, replica_groups=mesh['chip'=48,'core'=2,'zero'=8] {'zero'}, dimensions={0} | all-to-all | bytes 1441792 | tf_op jit(solution)/shard_map/all_to_all | solution.py:79
  130.2 7.4 %collective-permute-start.2 = (bf16[8,88,512]{2,1,0:T(8,128)(2,1)S(1)}, bf16[8,88,512]{2,1,0:T(8,128)(2,1)S(1)}, u32[]{:S(2)}, u32[]{:S(2)}) collective-permute-start(bf16[8,88,512]{2,1,0:T(8,128)(2,1)S(1)} %all_to_all.25), channel_id=1, source_target_pairs={{0,8},{8,0},{1,9},{9,1},{2,10},{10,2},{3,11},{11,3},{4,12},{12,4},... | collective-permute-start | bytes 2162696 | tf_op jit(solution)/shard_map/ppermute | solution.py:71
  137.6 1.6 collective-permute-done.2
  139.3 2.3 %convolution_convert_fusion.1 = bf16[704,704]{1,0:T(8,128)(2,1)} fusion(bf16[704,512]{1,0:T(8,128)(2,1)S(1)} %bitcast.36, bf16[704,512]{1,0:T(8,128)(2,1)S(1)} %bitcast.29, pred[]{:T(512)S(6)} %eq.38), kind=kOutput, calls=%fused_computation.5 | convolution fusion | flops 1022005248 | bytes 2433025 | tf_op jit(solution)/shard_map/dot_general | solution.py:24
  141.6 4.4 %add_convert_fusion = bf16[704,1024]{1,0:T(8,128)(2,1)S(1)} fusion(bf16[704,704]{1,0:T(8,128)(2,1)} %convolution_convert_fusion.1, bf16[704,512]{1,0:T(8,128)(2,1)S(1)} %bitcast.30, bf16[704,512]{1,0:T(8,128)(2,1)S(1)} %bitcast.37, pred[]{:T(512)S(6)} %eq.38), kind=kOutput, calls=%fused_computation.1 | convolution fusion | flops 1731186688 | bytes 3874817 | tf_op jit(solution)/shard_map/dot_general | solution.py:31
  146.0 0.0 copy-start.4
  146.0 1.1 copy-done.4
  147.1 1.3 convolution_convert_fusion
  148.4 4.1 %multiply_convert_fusion = bf16[704,1024]{1,0:T(8,128)(2,1)S(1)} fusion(bf16[704,1024]{1,0:T(8,128)(2,1)} %copy-done.4, bf16[704,704]{1,0:T(8,128)(2,1)S(1)} %convolution_convert_fusion), kind=kOutput, calls=%fused_computation | convolution fusion | flops 1718931456 | bytes 3874816 | tf_op jit(solution)/shard_map/dot_general | solution.py:31
  152.5 0.0 copy-start.2
  152.5 0.1 constant_dynamic-slice_fusion.5
  152.6 24.6 %all_to_all.26 = bf16[8,88,512]{2,1,0:T(8,128)(2,1)S(1)} all-to-all(bf16[8,88,512]{2,1,0:T(8,128)(2,1)S(1)} %constant_dynamic-slice_fusion.5), channel_id=1, replica_groups=mesh['chip'=48,'core'=2,'zero'=8] {'zero'}, dimensions={0} | all-to-all | bytes 1441792 | tf_op jit(solution)/shard_map/all_to_all | solution.py:82
  177.2 0.0 copy-done.2
  177.2 2.4 %collective-permute-start.3 = (bf16[8,88,512]{2,1,0:T(8,128)(2,1)S(1)}, bf16[8,88,512]{2,1,0:T(8,128)(2,1)S(1)}, u32[]{:S(2)}, u32[]{:S(2)}) collective-permute-start(bf16[8,88,512]{2,1,0:T(8,128)(2,1)S(1)} %all_to_all.26), channel_id=1, source_target_pairs={{0,8},{8,0},{1,9},{9,1},{2,10},{10,2},{3,11},{11,3},{4,12},{12,4},... | collective-permute-start | bytes 2162696 | tf_op jit(solution)/shard_map/ppermute | solution.py:71
  185.3 0.0 collective-permute-done.3
  185.3 0.4 maximum_select_fusion.1
  185.8 0.9 pad_maximum_fusion.1
  (7 shorter events, 0.2 us)
Async XLA Ops:
  3.2 13.5 %collective-permute-start = (bf16[48,2816]{1,0:T(8,128)(2,1)S(1)}, bf16[48,2816]{1,0:T(8,128)(2,1)S(1)}, u32[]{:S(2)}, u32[]{:S(2)}) collective-permute-start(bf16[48,2816]{1,0:T(8,128)(2,1)S(1)} %bitcast.34), channel_id=1, source_target_pairs={{0,8},{8,0},{1,9},{9,1},{2,10},{10,2},{3,11},{11,3},{4,12},{12,4},... | collective-permute-start | bytes 811016 | tf_op jit(solution)/shard_map/ppermute | solution.py:49
  17.2 11.1 %copy-start.1 = (f32[3,88,1024]{2,1,0:T(8,128)S(1)}, f32[3,88,1024]{2,1,0:T(8,128)}, u32[]{:S(2)}) copy-start(f32[3,88,1024]{2,1,0:T(8,128)} %param.4) | copy-start | bytes 3244036
  19.2 31.8 %all-to-all-start = ((bf16[48,2,2816]{2,1,0:T(2,128)(2,1)}), bf16[48,2,2816]{2,1,0:T(2,128)(2,1)S(1)}, u32[]{:S(2)}, u32[]{:S(2)}) async-start(bf16[48,2,2816]{2,1,0:T(2,128)(2,1)} %pad_maximum_fusion), calls=%async_computation | async-start | bytes 1081344 | tf_op jit(solution)/shard_map/all_to_all | solution.py:50
  51.5 37.3 %copy-start.3 = (s32[3]{0:T(128)S(1)}, s32[3]{0:T(128)}, u32[]{:S(2)}) copy-start(s32[3]{0:T(128)} %param.5) | copy-start | bytes 40
  83.8 7.6 %collective-permute-start.1 = (f32[48,2816]{1,0:T(8,128)S(1)}, f32[48,2816]{1,0:T(8,128)S(1)}, u32[]{:S(2)}, u32[]{:S(2)}) collective-permute-start(f32[48,2816]{1,0:T(8,128)S(1)} %bitcast.31), channel_id=1, source_target_pairs={{0,8},{8,0},{1,9},{9,1},{2,10},{10,2},{3,11},{11,3},{4,12},{12,4},... | collective-permute-start | bytes 1622024 | tf_op jit(solution)/shard_map/ppermute | solution.py:57
  94.2 14.3 %copy-start = (f32[3,88,1024]{2,1,0:T(8,128)}, f32[3,88,1024]{2,1,0:T(8,128)S(1)}, u32[]{:S(2)}) copy-start(f32[3,88,1024]{2,1,0:T(8,128)S(1)} %select_n.66) | copy-start | bytes 3244036
  130.2 9.0 %collective-permute-start.2 = (bf16[8,88,512]{2,1,0:T(8,128)(2,1)S(1)}, bf16[8,88,512]{2,1,0:T(8,128)(2,1)S(1)}, u32[]{:S(2)}, u32[]{:S(2)}) collective-permute-start(bf16[8,88,512]{2,1,0:T(8,128)(2,1)S(1)} %all_to_all.25), channel_id=1, source_target_pairs={{0,8},{8,0},{1,9},{9,1},{2,10},{10,2},{3,11},{11,3},{4,12},{12,4},... | collective-permute-start | bytes 2162696 | tf_op jit(solution)/shard_map/ppermute | solution.py:71
  146.0 1.1 copy-start.4
  152.5 24.6 %copy-start.2 = (bf16[704,1024]{1,0:T(8,128)(2,1)}, bf16[704,1024]{1,0:T(8,128)(2,1)S(1)}, u32[]{:S(2)}) copy-start(bf16[704,1024]{1,0:T(8,128)(2,1)S(1)} %multiply_convert_fusion) | copy-start | bytes 4325380
  177.2 8.1 %collective-permute-start.3 = (bf16[8,88,512]{2,1,0:T(8,128)(2,1)S(1)}, bf16[8,88,512]{2,1,0:T(8,128)(2,1)S(1)}, u32[]{:S(2)}, u32[]{:S(2)}) collective-permute-start(bf16[8,88,512]{2,1,0:T(8,128)(2,1)S(1)} %all_to_all.26), channel_id=1, source_target_pairs={{0,8},{8,0},{1,9},{9,1},{2,10},{10,2},{3,11},{11,3},{4,12},{12,4},... | collective-permute-start | bytes 2162696 | tf_op jit(solution)/shard_map/ppermute | solution.py:71

commit v7 on v5

--- a/solution.py
+++ b/solution.py
@@ -53,12 +53,8 @@
     other = lax.ppermute(mine, "core", [(0, 1), (1, 0)])
     ordered = jnp.where(core == 0, jnp.stack([mine, other], axis=1), jnp.stack([other, mine], axis=1))
     new_momentum = ordered.reshape(momentum.shape)
-    partial_value = jnp.sum(new_momentum * new_momentum, axis=(1, 2))
-    squares = lax.psum(partial_value, "zero")
-    inverse = 1.0 / (jnp.sqrt(squares) + NORM_EPSILON)
-    start_rows = (new_momentum * inverse[:, None, None]).astype(jnp.bfloat16)
     n_zero = lax.axis_size("zero")
-    width = start_rows.shape[-1] // 2
+    width = new_momentum.shape[-1] // 2
 
     def own_half(blocks):
         return lax.dynamic_slice_in_dim(blocks, core * width, width, axis=2)
@@ -68,18 +64,20 @@
         return jnp.where(core == 0, jnp.concatenate([mine, other], axis=2),
                          jnp.concatenate([other, mine], axis=2))
 
-    outgoing = jnp.zeros((n_zero,) + start_rows.shape[1:], start_rows.dtype)
+    outgoing = jnp.zeros((n_zero,) + new_momentum.shape[1:], new_momentum.dtype)
     owners = jnp.arange(n_zero, dtype=owner_table.dtype)[:, None, None]
-    for j in range(start_rows.shape[0]):
-        outgoing = jnp.where(owners == owner_table[j], start_rows[j][None], outgoing)
+    for j in range(new_momentum.shape[0]):
+        outgoing = jnp.where(owners == owner_table[j], new_momentum[j][None], outgoing)
     incoming = both_halves(lax.all_to_all(own_half(outgoing), "zero", 0, 0, tiled=True))
-    full_matrix = incoming.reshape(-1, incoming.shape[-1])
+    owned = incoming.reshape(-1, incoming.shape[-1])
+    norm = jnp.sqrt(jnp.sum(owned * owned))
+    full_matrix = (owned / (norm + NORM_EPSILON)).astype(jnp.bfloat16)
     result = orthogonalize(full_matrix)
     back = lax.all_to_all(own_half(result.reshape(incoming.shape)), "zero", 0, 0, tiled=True)
     returned = both_halves(back)
     update_rows = jnp.stack(
         [lax.dynamic_index_in_dim(returned, owner_table[j], 0, keepdims=False)
-         for j in range(start_rows.shape[0])]
+         for j in range(new_momentum.shape[0])]
     )
     return (new_momentum, update_rows, result[None])
 

time: 187 us -> 204 us (1.091)
  blocking collectives: 88.3 us -> 97.1 us
  local copies, waits for them, and re-layouts: 7.87 us -> 13 us
  starting transfers between devices: 34.4 us -> 29.7 us
  other arithmetic: 10.3 us -> 14 us
  matrix products: 12.2 us -> 14.5 us
    all_to_all x1, blocking collectives: 21.4 us -> 44.3 us  [on_device(): lax.all_to_all(own_half(outgoing), 'zero', 0, 0, tiled=True)]
    psum x1 -> x0, blocking collectives: 14 us -> none  [on_device(): squares = lax.psum(partial_value, 'zero')]
    ppermute x2, starting transfers between devices: 9.64 us -> 4.76 us  [both_halves(): other = lax.ppermute(mine, 'core', [(0, 1), (1, 0)])]
    unnamed x13 -> x15, local copies, waits for them, and re-layouts: 2.52 us -> 5.8 us
    convert_element_type x1, other arithmetic: 0.16 us -> 2.66 us  [on_device(): full_matrix = (owned / (norm + NORM_EPSILON)).astype(jnp.bfloat16)]
where the time goes in v7:
time: 204 us
  blocking collectives  97.1 us (48%)
  starting transfers between devices  29.7 us (15%)
  waiting for transfers between devices  28.3 us (14%)
  matrix products  14.5 us (7%)
  other arithmetic  14 us (7%)
  local copies, waits for them, and re-layouts  13 us (6%)
  between operations  7.08 us (3%)
    all_to_all x1, blocking collectives, on_device(): lax.all_to_all(own_half(outgoing), 'zero', 0, 0, tiled=True)  44.3 us
    all_to_all x1, blocking collectives, on_device(): mine = lax.all_to_all(spread, 'chip', 0, 0, tiled=True)  28.3 us
    all_to_all x1, waiting for transfers between devices, on_device(): lax.all_to_all(local_part.reshape(n_dp, chunk), DP, 0, 0, tiled=True)  25.4 us
    all_to_all x1, blocking collectives, on_device(): lax.all_to_all(own_half(result.reshape(incoming.shape)), 'zero', 0, 0, ti...  24.6 us
    all_to_all x1, starting transfers between devices, on_device(): lax.all_to_all(local_part.reshape(n_dp, chunk), DP, 0, 0, tiled=True)  20.1 us
    dot_general x2, matrix products, orthogonalize(): jnp.dot(poly_term, current, preferred_element_type=jnp.float32)  9.91 us
    unnamed x15, local copies, waits for them, and re-layouts  5.8 us
    ppermute x1, starting transfers between devices, on_device(): other = lax.ppermute(mine, 'core', [(0, 1), (1, 0)])  4.78 us
  transfers between devices with their start and end apart: 4, of which 2 were waited for; matrix products, arithmetic and copies ran while one was open for 2% of the time, Pallas kernels for 0%

profile of v7, /device:TPU:1, one launch (start us, length us, event | category | flops | bytes accessed | tf_op | source)
XLA Modules:
  0.0 203.6 jit_solution(13041076186358830996)
XLA Ops:
  0.6 2.1 %all_to_all.24 = bf16[96,1,2816]{2,1,0:T(2,128)(2,1)S(1)} reshape(bf16[1,3,88,1024]{3,2,1,0:T(8,128)(2,1)} %param.3) | data formatting | bytes 1081344 | tf_op jit(solution)/shard_map/all_to_all | solution.py:46
  2.8 0.5 broadcast.50
  3.3 3.9 %reduce.3 = bf16[96,2816]{1,0:T(8,128)(2,1)S(1)} reduce(bf16[96,1,2816]{2,1,0:T(2,128)(2,1)S(1)} %all_to_all.24, bf16[]{:T(256)} %broadcast.50), dimensions={1}, to_apply=%all_to_all.24.reduce_sub_computation | reduce | bytes 1081346 | tf_op jit(solution)/shard_map/all_to_all | solution.py:46
  7.2 0.9 reshape.57
  8.1 20.1 %all-to-all-start = ((bf16[96,2,1408]{2,1,0:T(2,128)(2,1)}), bf16[96,2,1408]{2,1,0:T(2,128)(2,1)S(1)}, u32[]{:S(2)}, u32[]{:S(2)}) async-start(bf16[96,2,1408]{2,1,0:T(2,128)(2,1)} %reshape.57), calls=%async_computation | async-start | bytes 1081344 | tf_op jit(solution)/shard_map/all_to_all | solution.py:46
  28.3 0.0 copy-done.2
  28.3 0.4 reshape.54
  28.7 25.4 %all-to-all-done = bf16[96,2,1408]{2,1,0:T(2,128)(2,1)S(1)} async-done(((bf16[96,2,1408]{2,1,0:T(2,128)(2,1)}), bf16[96,2,1408]{2,1,0:T(2,128)(2,1)S(1)}, u32[]{:S(2)}, u32[]{:S(2)}) %all-to-all-start) | async-done | bytes 540704 | tf_op jit(solution)/shard_map/all_to_all | solution.py:46
  54.1 0.4 reshape.58
  54.6 1.0 convert_reduce_fusion
  55.7 0.3 broadcast_in_dim.58
  55.9 28.3 %all_to_all.29 = f32[48,1,2816]{2,1,0:T(1,128)S(1)} all-to-all(f32[48,1,2816]{2,1,0:T(1,128)S(1)} %broadcast_in_dim.58), channel_id=1, replica_groups=mesh['chip'=48,'core'=2,'zero'=8] {'chip'}, dimensions={0} | all-to-all | bytes 1081344 | tf_op jit(solution)/shard_map/all_to_all | solution.py:52
  84.3 4.8 %collective-permute-start = (f32[48,2816]{1,0:T(8,128)S(1)}, f32[48,2816]{1,0:T(8,128)S(1)}, u32[]{:S(2)}, u32[]{:S(2)}) collective-permute-start(f32[48,2816]{1,0:T(8,128)S(1)} %bitcast.26), channel_id=1, source_target_pairs={{0,8},{8,0},{1,9},{9,1},{2,10},{10,2},{3,11},{11,3},{4,12},{12,4},... | collective-permute-start | bytes 1622024 | tf_op jit(solution)/shard_map/ppermute | solution.py:53
  89.0 0.0 copy-done.4
  89.1 0.6 fusion.5
  89.6 0.6 iota_compare_fusion.2
  90.3 1.2 iota_compare_fusion
  91.5 0.0 collective-permute-done
  91.5 0.4 stack.8
  91.9 1.5 maximum_select_fusion.2
  93.4 0.1 fusion.4
  93.5 0.3 broadcast_in_dim.66
  93.8 0.3 broadcast_in_dim.63
  94.1 0.3 broadcast_in_dim.60
  94.5 0.3 select_select_fusion
  94.8 44.3 %all_to_all.30 = f32[8,88,512]{2,1,0:T(8,128)S(1)} all-to-all(f32[8,88,512]{2,1,0:T(8,128)S(1)} %select_select_fusion), channel_id=1, replica_groups=mesh['chip'=48,'core'=2,'zero'=8] {'zero'}, dimensions={0} | all-to-all | bytes 2883584 | tf_op jit(solution)/shard_map/all_to_all | solution.py:71
  139.1 2.4 %collective-permute-start.1 = (f32[8,88,512]{2,1,0:T(8,128)S(1)}, f32[8,88,512]{2,1,0:T(8,128)S(1)}, u32[]{:S(2)}, u32[]{:S(2)}) collective-permute-start(f32[8,88,512]{2,1,0:T(8,128)S(1)} %all_to_all.30), channel_id=1, source_target_pairs={{0,8},{8,0},{1,9},{9,1},{2,10},{10,2},{3,11},{11,3},{4,12},{12,4},... | collective-permute-start | bytes 4325384 | tf_op jit(solution)/shard_map/ppermute | solution.py:63
  141.4 2.8 %collective-permute-done.1 = f32[8,88,512]{2,1,0:T(8,128)S(1)} collective-permute-done((f32[8,88,512]{2,1,0:T(8,128)S(1)}, f32[8,88,512]{2,1,0:T(8,128)S(1)}, u32[]{:S(2)}, u32[]{:S(2)}) %collective-permute-start.1) | collective-permute-done | bytes 1441824 | tf_op jit(solution)/shard_map/ppermute | solution.py:63
  144.3 1.1 copy-done
  145.4 1.4 multiply_reduce_fusion
  147.5 2.7 %divide_convert_fusion = bf16[704,1024]{1,0:T(8,128)(2,1)S(1)} fusion(f32[704,512]{1,0:T(8,128)S(1)} %bitcast.23, f32[704,512]{1,0:T(8,128)} %bitcast.25, f32[]{:T(128)S(6)} %add.45, pred[]{:T(512)S(6)} %eq.38), kind=kLoop, calls=%fused_computation.3 | loop fusion | flops 3604480 | bytes 4325381 | tf_op jit(solution)/shard_map/convert_element_type | solution.py:74
  150.1 0.0 copy-start.1
  150.1 1.1 copy-done.1
  151.2 2.3 %convolution_convert_fusion.1 = bf16[704,704]{1,0:T(8,128)(2,1)} fusion(bf16[704,1024]{1,0:T(8,128)(2,1)S(1)} %divide_convert_fusion), kind=kOutput, calls=%fused_computation.8 | convolution fusion | flops 1015517184 | bytes 2433024 | tf_op jit(solution)/shard_map/dot_general | solution.py:24
  153.5 4.9 %add_convert_fusion = bf16[704,1024]{1,0:T(8,128)(2,1)S(1)} fusion(bf16[704,1024]{1,0:T(8,128)(2,1)} %copy-done.1, bf16[704,704]{1,0:T(8,128)(2,1)} %convolution_convert_fusion.1), kind=kOutput, calls=%fused_computation.2 | convolution fusion | flops 1718210560 | bytes 3874816 | tf_op jit(solution)/shard_map/dot_general | solution.py:31
  158.5 0.0 copy-start.5
  158.5 1.1 copy-done.5
  159.6 2.3 %convolution_convert_fusion = bf16[704,704]{1,0:T(8,128)(2,1)} fusion(bf16[704,1024]{1,0:T(8,128)(2,1)S(1)} %add_convert_fusion), kind=kOutput, calls=%fused_computation.7 | convolution fusion | flops 1015517184 | bytes 2433024 | tf_op jit(solution)/shard_map/dot_general | solution.py:24
  161.9 5.0 %multiply_convert_fusion = bf16[704,1024]{1,0:T(8,128)(2,1)S(1)} fusion(bf16[704,1024]{1,0:T(8,128)(2,1)} %copy-done.5, bf16[704,704]{1,0:T(8,128)(2,1)} %convolution_convert_fusion), kind=kOutput, calls=%fused_computation.1 | convolution fusion | flops 1718931456 | bytes 3874816 | tf_op jit(solution)/shard_map/dot_general | solution.py:31
  166.9 0.0 copy-start.3
  166.9 1.1 copy-done.3
  168.0 0.1 constant_dynamic-slice_fusion.5
  168.0 24.6 %all_to_all.31 = bf16[8,88,512]{2,1,0:T(8,128)(2,1)S(1)} all-to-all(bf16[8,88,512]{2,1,0:T(8,128)(2,1)S(1)} %constant_dynamic-slice_fusion.5), channel_id=1, replica_groups=mesh['chip'=48,'core'=2,'zero'=8] {'zero'}, dimensions={0} | all-to-all | bytes 1441792 | tf_op jit(solution)/shard_map/all_to_all | solution.py:76
  192.6 2.4 %collective-permute-start.2 = (bf16[8,88,512]{2,1,0:T(8,128)(2,1)S(1)}, bf16[8,88,512]{2,1,0:T(8,128)(2,1)S(1)}, u32[]{:S(2)}, u32[]{:S(2)}) collective-permute-start(bf16[8,88,512]{2,1,0:T(8,128)(2,1)S(1)} %all_to_all.31), channel_id=1, source_target_pairs={{0,8},{8,0},{1,9},{9,1},{2,10},{10,2},{3,11},{11,3},{4,12},{12,4},... | collective-permute-start | bytes 2162696 | tf_op jit(solution)/shard_map/ppermute | solution.py:63
  200.5 1.8 select_n.59
  202.3 0.0 collective-permute-done.2
  202.3 0.4 maximum_select_fusion.1
  202.8 0.9 pad_maximum_fusion
  (8 shorter events, 0.2 us)
Async XLA Ops:
  8.1 20.2 %copy-start.2 = (f32[3,88,1024]{2,1,0:T(8,128)S(1)}, f32[3,88,1024]{2,1,0:T(8,128)}, u32[]{:S(2)}) copy-start(f32[3,88,1024]{2,1,0:T(8,128)} %param.4) | copy-start | bytes 3244036
  8.1 46.0 %all-to-all-start = ((bf16[96,2,1408]{2,1,0:T(2,128)(2,1)}), bf16[96,2,1408]{2,1,0:T(2,128)(2,1)S(1)}, u32[]{:S(2)}, u32[]{:S(2)}) async-start(bf16[96,2,1408]{2,1,0:T(2,128)(2,1)} %reshape.57), calls=%async_computation | async-start | bytes 1081344 | tf_op jit(solution)/shard_map/all_to_all | solution.py:46
  55.6 33.4 %copy-start.4 = (s32[3]{0:T(128)S(1)}, s32[3]{0:T(128)}, u32[]{:S(2)}) copy-start(s32[3]{0:T(128)} %param.5) | copy-start | bytes 40
  84.3 7.2 %collective-permute-start = (f32[48,2816]{1,0:T(8,128)S(1)}, f32[48,2816]{1,0:T(8,128)S(1)}, u32[]{:S(2)}, u32[]{:S(2)}) collective-permute-start(f32[48,2816]{1,0:T(8,128)S(1)} %bitcast.26), channel_id=1, source_target_pairs={{0,8},{8,0},{1,9},{9,1},{2,10},{10,2},{3,11},{11,3},{4,12},{12,4},... | collective-permute-start | bytes 1622024 | tf_op jit(solution)/shard_map/ppermute | solution.py:53
  139.1 5.2 %collective-permute-start.1 = (f32[8,88,512]{2,1,0:T(8,128)S(1)}, f32[8,88,512]{2,1,0:T(8,128)S(1)}, u32[]{:S(2)}, u32[]{:S(2)}) collective-permute-start(f32[8,88,512]{2,1,0:T(8,128)S(1)} %all_to_all.30), channel_id=1, source_target_pairs={{0,8},{8,0},{1,9},{9,1},{2,10},{10,2},{3,11},{11,3},{4,12},{12,4},... | collective-permute-start | bytes 4325384 | tf_op jit(solution)/shard_map/ppermute | solution.py:63
  144.3 1.1 copy-start
  150.1 1.1 copy-start.1
  158.5 1.1 copy-start.5
  166.9 1.1 copy-start.3
  192.6 9.7 %collective-permute-start.2 = (bf16[8,88,512]{2,1,0:T(8,128)(2,1)S(1)}, bf16[8,88,512]{2,1,0:T(8,128)(2,1)S(1)}, u32[]{:S(2)}, u32[]{:S(2)}) collective-permute-start(bf16[8,88,512]{2,1,0:T(8,128)(2,1)S(1)} %all_to_all.31), channel_id=1, source_target_pairs={{0,8},{8,0},{1,9},{9,1},{2,10},{10,2},{3,11},{11,3},{4,12},{12,4},... | collective-permute-start | bytes 2162696 | tf_op jit(solution)/shard_map/ppermute | solution.py:63

commit v8 on v5

--- a/solution.py
+++ b/solution.py
@@ -54,7 +54,9 @@
     ordered = jnp.where(core == 0, jnp.stack([mine, other], axis=1), jnp.stack([other, mine], axis=1))
     new_momentum = ordered.reshape(momentum.shape)
     partial_value = jnp.sum(new_momentum * new_momentum, axis=(1, 2))
-    squares = lax.psum(partial_value, "zero")
+    n_zero = lax.axis_size("zero")
+    spread_sums = jnp.broadcast_to(partial_value[None], (n_zero,) + partial_value.shape)
+    squares = jnp.sum(lax.all_to_all(spread_sums, "zero", 0, 0, tiled=True), axis=0)
     inverse = 1.0 / (jnp.sqrt(squares) + NORM_EPSILON)
     start_rows = (new_momentum * inverse[:, None, None]).astype(jnp.bfloat16)
     n_zero = lax.axis_size("zero")

time: 187 us -> 186 us (level)
  blocking collectives: 88.3 us -> 75.1 us
  waiting for transfers between devices: 27.2 us -> 33.7 us
  starting transfers between devices: 34.4 us -> 38.7 us
    psum x1 -> x0, blocking collectives: 14 us -> none  [on_device(): squares = lax.psum(partial_value, 'zero')]
    all_to_all x0 -> x1, starting transfers between devices: none -> 6.82 us  [on_device(): lax.all_to_all(spread_sums, 'zero', 0, 0, tiled=True)]
    all_to_all x0 -> x1, waiting for transfers between devices: none -> 6.48 us  [on_device(): lax.all_to_all(spread_sums, 'zero', 0, 0, tiled=True)]
    ppermute x2, starting transfers between devices: 9.64 us -> 7.09 us  [both_halves(): other = lax.ppermute(mine, 'core', [(0, 1), (1, 0)])]
  transfers between devices with their start and end apart: 4 -> 5, of which waited for: 2 -> 3; matrix products, arithmetic and copies ran while one was open for 2% -> 2% of each run, Pallas kernels for 0% -> 0%
where the time goes in v8:
time: 186 us; the launch traced here: 185 us
  blocking collectives  75.1 us (40%)
  starting transfers between devices  38.7 us (21%)
  waiting for transfers between devices  33.7 us (18%)
  matrix products  12.2 us (7%)
  other arithmetic  10.3 us (6%)
  local copies, waits for them, and re-layouts  8.6 us (5%)
  between operations  6.51 us (4%)
    all_to_all x1, blocking collectives, on_device(): mine = lax.all_to_all(spread, 'chip', 0, 0, tiled=True)  28.3 us
    all_to_all x1, waiting for transfers between devices, on_device(): lax.all_to_all(local_part.reshape(n_dp, chunk), DP, 0, 0, tiled=True)  25.4 us
    all_to_all x1, blocking collectives, on_device(): lax.all_to_all(own_half(result.reshape(incoming.shape)), 'zero', 0, 0, ti...  24.5 us
    all_to_all x1, blocking collectives, on_device(): lax.all_to_all(own_half(outgoing), 'zero', 0, 0, tiled=True)  22.3 us
    all_to_all x1, starting transfers between devices, on_device(): lax.all_to_all(local_part.reshape(n_dp, chunk), DP, 0, 0, tiled=True)  20 us
    dot_general x2, matrix products, orthogonalize(): jnp.dot(poly_term, current, preferred_element_type=jnp.float32)  8.53 us
    ppermute x2, starting transfers between devices, both_halves(): other = lax.ppermute(mine, 'core', [(0, 1), (1, 0)])  7.09 us
    all_to_all x1, starting transfers between devices, on_device(): lax.all_to_all(spread_sums, 'zero', 0, 0, tiled=True)  6.82 us
  transfers between devices with their start and end apart: 5, of which 3 were waited for; matrix products, arithmetic and copies ran while one was open for 2% of the time, Pallas kernels for 0%

profile of v8, /device:TPU:1, one launch (start us, length us, event | category | flops | bytes accessed | tf_op | source)
XLA Modules:
  0.0 185.1 jit_solution(8198757164164262281)
XLA Ops:
  0.6 2.1 %all_to_all.29 = bf16[96,1,2816]{2,1,0:T(2,128)(2,1)S(1)} reshape(bf16[1,3,88,1024]{3,2,1,0:T(8,128)(2,1)} %param.3) | data formatting | bytes 1081344 | tf_op jit(solution)/shard_map/all_to_all | solution.py:46
  2.8 0.5 broadcast.71
  3.3 3.9 %reduce.4 = bf16[96,2816]{1,0:T(8,128)(2,1)S(1)} reduce(bf16[96,1,2816]{2,1,0:T(2,128)(2,1)S(1)} %all_to_all.29, bf16[]{:T(256)} %broadcast.71), dimensions={1}, to_apply=%all_to_all.29.reduce_sub_computation | reduce | bytes 1081346 | tf_op jit(solution)/shard_map/all_to_all | solution.py:46
  7.2 0.0 copy-start.1
  7.2 0.9 reshape.62
  8.1 20.0 %all-to-all-start = ((bf16[96,2,1408]{2,1,0:T(2,128)(2,1)}), bf16[96,2,1408]{2,1,0:T(2,128)(2,1)S(1)}, u32[]{:S(2)}, u32[]{:S(2)}) async-start(bf16[96,2,1408]{2,1,0:T(2,128)(2,1)} %reshape.62), calls=%async_computation | async-start | bytes 1081344 | tf_op jit(solution)/shard_map/all_to_all | solution.py:46
  28.1 0.0 copy-done.1
  28.2 0.4 reshape.59
  28.5 25.4 %all-to-all-done = bf16[96,2,1408]{2,1,0:T(2,128)(2,1)S(1)} async-done(((bf16[96,2,1408]{2,1,0:T(2,128)(2,1)}), bf16[96,2,1408]{2,1,0:T(2,128)(2,1)S(1)}, u32[]{:S(2)}, u32[]{:S(2)}) %all-to-all-start) | async-done | bytes 540704 | tf_op jit(solution)/shard_map/all_to_all | solution.py:46
  54.0 0.4 reshape.63
  54.4 1.0 convert_reduce_fusion
  55.5 0.0 copy-start.3
  55.5 0.3 broadcast_in_dim.65
  55.8 28.3 %all_to_all.35 = f32[48,1,2816]{2,1,0:T(1,128)S(1)} all-to-all(f32[48,1,2816]{2,1,0:T(1,128)S(1)} %broadcast_in_dim.65), channel_id=1, replica_groups=mesh['chip'=48,'core'=2,'zero'=8] {'chip'}, dimensions={0} | all-to-all | bytes 1081344 | tf_op jit(solution)/shard_map/all_to_all | solution.py:52
  84.1 4.8 %collective-permute-start = (f32[48,2816]{1,0:T(8,128)S(1)}, f32[48,2816]{1,0:T(8,128)S(1)}, u32[]{:S(2)}, u32[]{:S(2)}) collective-permute-start(f32[48,2816]{1,0:T(8,128)S(1)} %bitcast.27), channel_id=1, source_target_pairs={{0,8},{8,0},{1,9},{9,1},{2,10},{10,2},{3,11},{11,3},{4,12},{12,4},... | collective-permute-start | bytes 1622024 | tf_op jit(solution)/shard_map/ppermute | solution.py:53
  88.9 0.0 copy-done.3
  88.9 0.6 fusion.6
  89.5 0.6 iota_compare_fusion.2
  90.2 1.3 iota_compare_fusion
  91.4 0.0 collective-permute-done
  91.4 0.4 stack.8
  91.8 1.5 maximum_select_fusion.2
  93.4 0.9 select_n.57
  94.2 0.0 copy-start
  94.2 0.2 multiply_reduce_fusion
  94.5 0.7 broadcast_in_dim.67
  95.2 6.8 %all-to-all-start.2 = ((f32[8,1,3]{2,1,0:T(1,128)}), f32[8,1,3]{2,1,0:T(1,128)S(1)}, u32[]{:S(2)}, u32[]{:S(2)}) async-start(f32[8,1,3]{2,1,0:T(1,128)} %broadcast_in_dim.67), calls=%async_computation.2 | async-start | bytes 8192 | tf_op jit(solution)/shard_map/all_to_all | solution.py:59
  102.0 6.5 %all-to-all-done.2 = f32[8,1,3]{2,1,0:T(1,128)S(1)} async-done(((f32[8,1,3]{2,1,0:T(1,128)}), f32[8,1,3]{2,1,0:T(1,128)S(1)}, u32[]{:S(2)}, u32[]{:S(2)}) %all-to-all-start.2) | async-done | bytes 128 | tf_op jit(solution)/shard_map/all_to_all | solution.py:59
  108.5 0.2 multiply_convert_fusion.1
  108.7 0.0 copy-done
  108.8 0.3 select_select_fusion
  109.1 22.3 %all_to_all.36 = bf16[8,88,512]{2,1,0:T(8,128)(2,1)S(1)} all-to-all(bf16[8,88,512]{2,1,0:T(8,128)(2,1)S(1)} %select_select_fusion), channel_id=1, replica_groups=mesh['chip'=48,'core'=2,'zero'=8] {'zero'}, dimensions={0} | all-to-all | bytes 1441792 | tf_op jit(solution)/shard_map/all_to_all | solution.py:77
  131.3 4.7 %collective-permute-start.1 = (bf16[8,88,512]{2,1,0:T(8,128)(2,1)S(1)}, bf16[8,88,512]{2,1,0:T(8,128)(2,1)S(1)}, u32[]{:S(2)}, u32[]{:S(2)}) collective-permute-start(bf16[8,88,512]{2,1,0:T(8,128)(2,1)S(1)} %all_to_all.36), channel_id=1, source_target_pairs={{0,8},{8,0},{1,9},{9,1},{2,10},{10,2},{3,11},{11,3},{4,12},{12,4},... | collective-permute-start | bytes 2162696 | tf_op jit(solution)/shard_map/ppermute | solution.py:69
  136.0 1.8 collective-permute-done.1
  137.8 2.3 %convolution_convert_fusion.1 = bf16[704,704]{1,0:T(8,128)(2,1)} fusion(bf16[704,512]{1,0:T(8,128)(2,1)S(1)} %bitcast.30, bf16[704,512]{1,0:T(8,128)(2,1)S(1)} %bitcast.25, pred[]{:T(512)S(6)} %eq.38), kind=kOutput, calls=%fused_computation.5 | convolution fusion | flops 1022005248 | bytes 2433025 | tf_op jit(solution)/shard_map/dot_general | solution.py:24
  140.1 4.4 %add_convert_fusion = bf16[704,1024]{1,0:T(8,128)(2,1)S(1)} fusion(bf16[704,704]{1,0:T(8,128)(2,1)} %convolution_convert_fusion.1, bf16[704,512]{1,0:T(8,128)(2,1)S(1)} %bitcast.26, bf16[704,512]{1,0:T(8,128)(2,1)S(1)} %bitcast.31, pred[]{:T(512)S(6)} %eq.38), kind=kOutput, calls=%fused_computation.1 | convolution fusion | flops 1731186688 | bytes 3874817 | tf_op jit(solution)/shard_map/dot_general | solution.py:31
  144.6 0.0 copy-start.4
  144.6 1.1 copy-done.4
  145.7 1.3 convolution_convert_fusion
  147.0 4.1 %multiply_convert_fusion = bf16[704,1024]{1,0:T(8,128)(2,1)S(1)} fusion(bf16[704,1024]{1,0:T(8,128)(2,1)} %copy-done.4, bf16[704,704]{1,0:T(8,128)(2,1)S(1)} %convolution_convert_fusion), kind=kOutput, calls=%fused_computation | convolution fusion | flops 1718931456 | bytes 3874816 | tf_op jit(solution)/shard_map/dot_general | solution.py:31
  151.1 0.0 copy-start.2
  151.1 0.1 constant_dynamic-slice_fusion.5
  151.2 24.5 %all_to_all.37 = bf16[8,88,512]{2,1,0:T(8,128)(2,1)S(1)} all-to-all(bf16[8,88,512]{2,1,0:T(8,128)(2,1)S(1)} %constant_dynamic-slice_fusion.5), channel_id=1, replica_groups=mesh['chip'=48,'core'=2,'zero'=8] {'zero'}, dimensions={0} | all-to-all | bytes 1441792 | tf_op jit(solution)/shard_map/all_to_all | solution.py:80
  175.8 0.0 copy-done.2
  175.8 2.4 %collective-permute-start.2 = (bf16[8,88,512]{2,1,0:T(8,128)(2,1)S(1)}, bf16[8,88,512]{2,1,0:T(8,128)(2,1)S(1)}, u32[]{:S(2)}, u32[]{:S(2)}) collective-permute-start(bf16[8,88,512]{2,1,0:T(8,128)(2,1)S(1)} %all_to_all.37), channel_id=1, source_target_pairs={{0,8},{8,0},{1,9},{9,1},{2,10},{10,2},{3,11},{11,3},{4,12},{12,4},... | collective-permute-start | bytes 2162696 | tf_op jit(solution)/shard_map/ppermute | solution.py:69
  183.7 0.0 collective-permute-done.2
  183.8 0.4 maximum_select_fusion.1
  184.2 0.9 pad_maximum_fusion
  (8 shorter events, 0.2 us)
Async XLA Ops:
  7.2 21.0 %copy-start.1 = (f32[3,88,1024]{2,1,0:T(8,128)S(1)}, f32[3,88,1024]{2,1,0:T(8,128)}, u32[]{:S(2)}) copy-start(f32[3,88,1024]{2,1,0:T(8,128)} %param.4) | copy-start | bytes 3244036
  8.1 45.9 %all-to-all-start = ((bf16[96,2,1408]{2,1,0:T(2,128)(2,1)}), bf16[96,2,1408]{2,1,0:T(2,128)(2,1)S(1)}, u32[]{:S(2)}, u32[]{:S(2)}) async-start(bf16[96,2,1408]{2,1,0:T(2,128)(2,1)} %reshape.62), calls=%async_computation | async-start | bytes 1081344 | tf_op jit(solution)/shard_map/all_to_all | solution.py:46
  55.5 33.4 %copy-start.3 = (s32[3]{0:T(128)S(1)}, s32[3]{0:T(128)}, u32[]{:S(2)}) copy-start(s32[3]{0:T(128)} %param.5) | copy-start | bytes 40
  84.1 7.3 %collective-permute-start = (f32[48,2816]{1,0:T(8,128)S(1)}, f32[48,2816]{1,0:T(8,128)S(1)}, u32[]{:S(2)}, u32[]{:S(2)}) collective-permute-start(f32[48,2816]{1,0:T(8,128)S(1)} %bitcast.27), channel_id=1, source_target_pairs={{0,8},{8,0},{1,9},{9,1},{2,10},{10,2},{3,11},{11,3},{4,12},{12,4},... | collective-permute-start | bytes 1622024 | tf_op jit(solution)/shard_map/ppermute | solution.py:53
  94.2 14.5 %copy-start = (f32[3,88,1024]{2,1,0:T(8,128)}, f32[3,88,1024]{2,1,0:T(8,128)S(1)}, u32[]{:S(2)}) copy-start(f32[3,88,1024]{2,1,0:T(8,128)S(1)} %select_n.57) | copy-start | bytes 3244036
  95.2 13.3 %all-to-all-start.2 = ((f32[8,1,3]{2,1,0:T(1,128)}), f32[8,1,3]{2,1,0:T(1,128)S(1)}, u32[]{:S(2)}, u32[]{:S(2)}) async-start(f32[8,1,3]{2,1,0:T(1,128)} %broadcast_in_dim.67), calls=%async_computation.2 | async-start | bytes 8192 | tf_op jit(solution)/shard_map/all_to_all | solution.py:59
  131.3 6.5 %collective-permute-start.1 = (bf16[8,88,512]{2,1,0:T(8,128)(2,1)S(1)}, bf16[8,88,512]{2,1,0:T(8,128)(2,1)S(1)}, u32[]{:S(2)}, u32[]{:S(2)}) collective-permute-start(bf16[8,88,512]{2,1,0:T(8,128)(2,1)S(1)} %all_to_all.36), channel_id=1, source_target_pairs={{0,8},{8,0},{1,9},{9,1},{2,10},{10,2},{3,11},{11,3},{4,12},{12,4},... | collective-permute-start | bytes 2162696 | tf_op jit(solution)/shard_map/ppermute | solution.py:69
  144.6 1.1 copy-start.4
  151.1 24.6 %copy-start.2 = (bf16[704,1024]{1,0:T(8,128)(2,1)}, bf16[704,1024]{1,0:T(8,128)(2,1)S(1)}, u32[]{:S(2)}) copy-start(bf16[704,1024]{1,0:T(8,128)(2,1)S(1)} %multiply_convert_fusion) | copy-start | bytes 4325380
  175.8 8.0 %collective-permute-start.2 = (bf16[8,88,512]{2,1,0:T(8,128)(2,1)S(1)}, bf16[8,88,512]{2,1,0:T(8,128)(2,1)S(1)}, u32[]{:S(2)}, u32[]{:S(2)}) collective-permute-start(bf16[8,88,512]{2,1,0:T(8,128)(2,1)S(1)} %all_to_all.37), channel_id=1, source_target_pairs={{0,8},{8,0},{1,9},{9,1},{2,10},{10,2},{3,11},{11,3},{4,12},{12,4},... | collective-permute-start | bytes 2162696 | tf_op jit(solution)/shard_map/ppermute | solution.py:69

commit v9 on v8

--- a/solution.py
+++ b/solution.py
@@ -60,12 +60,18 @@
     inverse = 1.0 / (jnp.sqrt(squares) + NORM_EPSILON)
     start_rows = (new_momentum * inverse[:, None, None]).astype(jnp.bfloat16)
     n_zero = lax.axis_size("zero")
-    width = start_rows.shape[-1] // 2
+    quarter = core * 2 + lax.axis_index("chip") % 2
+    width = start_rows.shape[-1] // 4
+    neighbours = [(k, k ^ 1) for k in range(n_chip)]
 
     def own_half(blocks):
-        return lax.dynamic_slice_in_dim(blocks, core * width, width, axis=2)
+        return lax.dynamic_slice_in_dim(blocks, quarter * width, width, axis=2)
 
     def both_halves(mine):
+        pair_bit = lax.axis_index("chip") % 2
+        across = lax.ppermute(mine, "chip", neighbours)
+        mine = jnp.where(pair_bit == 0, jnp.concatenate([mine, across], axis=2),
+                         jnp.concatenate([across, mine], axis=2))
         other = lax.ppermute(mine, "core", [(0, 1), (1, 0)])
         return jnp.where(core == 0, jnp.concatenate([mine, other], axis=2),
                          jnp.concatenate([other, mine], axis=2))

time: 186 us -> 192 us (1.032)
  blocking collectives: 75.1 us -> 58.8 us
  waiting for transfers between devices: 33.7 us -> 47.8 us
  starting transfers between devices: 38.7 us -> 46.6 us
    ppermute x0 -> x2, waiting for transfers between devices: none -> 14.2 us  [both_halves(): across = lax.ppermute(mine, 'chip', neighbours)]
    all_to_all x1, blocking collectives: 24.5 us -> 15.9 us  [on_device(): lax.all_to_all(own_half(result.reshape(incoming.shape)), 'zero', 0, 0, ti...]
    all_to_all x1, blocking collectives: 22.3 us -> 14.7 us  [on_device(): lax.all_to_all(own_half(outgoing), 'zero', 0, 0, tiled=True)]
    ppermute x0 -> x2, starting transfers between devices: none -> 5 us  [both_halves(): across = lax.ppermute(mine, 'chip', neighbours)]
    ppermute x2, starting transfers between devices: 7.09 us -> 10 us  [both_halves(): other = lax.ppermute(mine, 'core', [(0, 1), (1, 0)])]
    dot_general x2, matrix products: 3.63 us -> 5.72 us  [orthogonalize(): jnp.dot(current, current.T, preferred_element_type=jnp.float32)]
  transfers between devices with their start and end apart: 5 -> 7, of which waited for: 3 -> 5; matrix products, arithmetic and copies ran while one was open for 2% -> 2% of each run, Pallas kernels for 0% -> 0%
where the time goes in v9:
time: 192 us; the launch traced here: 191 us
  blocking collectives  58.8 us (31%)
  waiting for transfers between devices  47.8 us (25%)
  starting transfers between devices  46.6 us (24%)
  matrix products  13.3 us (7%)
  other arithmetic  10.7 us (6%)
  local copies, waits for them, and re-layouts  7.52 us (4%)
  between operations  6.6 us (3%)
    all_to_all x1, blocking collectives, on_device(): mine = lax.all_to_all(spread, 'chip', 0, 0, tiled=True)  28.3 us
    all_to_all x1, waiting for transfers between devices, on_device(): lax.all_to_all(local_part.reshape(n_dp, chunk), DP, 0, 0, tiled=True)  25.4 us
    all_to_all x1, starting transfers between devices, on_device(): lax.all_to_all(local_part.reshape(n_dp, chunk), DP, 0, 0, tiled=True)  20 us
    all_to_all x1, blocking collectives, on_device(): lax.all_to_all(own_half(result.reshape(incoming.shape)), 'zero', 0, 0, ti...  15.9 us
    all_to_all x1, blocking collectives, on_device(): lax.all_to_all(own_half(outgoing), 'zero', 0, 0, tiled=True)  14.7 us
    ppermute x2, waiting for transfers between devices, both_halves(): across = lax.ppermute(mine, 'chip', neighbours)  14.2 us
    ppermute x2, starting transfers between devices, both_halves(): other = lax.ppermute(mine, 'core', [(0, 1), (1, 0)])  10 us
    dot_general x2, matrix products, orthogonalize(): jnp.dot(poly_term, current, preferred_element_type=jnp.float32)  7.6 us
  transfers between devices with their start and end apart: 7, of which 5 were waited for; matrix products, arithmetic and copies ran while one was open for 2% of the time, Pallas kernels for 0%

profile of v9, /device:TPU:1, one launch (start us, length us, event | category | flops | bytes accessed | tf_op | source)
XLA Modules:
  0.0 191.4 jit_solution(9362365269075324978)
XLA Ops:
  0.6 2.1 %all_to_all.29 = bf16[96,1,2816]{2,1,0:T(2,128)(2,1)S(1)} reshape(bf16[1,3,88,1024]{3,2,1,0:T(8,128)(2,1)} %param.3) | data formatting | bytes 1081344 | tf_op jit(solution)/shard_map/all_to_all | solution.py:46
  2.8 0.5 broadcast.73
  3.3 3.9 %reduce.4 = bf16[96,2816]{1,0:T(8,128)(2,1)S(1)} reduce(bf16[96,1,2816]{2,1,0:T(2,128)(2,1)S(1)} %all_to_all.29, bf16[]{:T(256)} %broadcast.73), dimensions={1}, to_apply=%all_to_all.29.reduce_sub_computation | reduce | bytes 1081346 | tf_op jit(solution)/shard_map/all_to_all | solution.py:46
  7.2 0.0 copy-start.1
  7.2 0.9 reshape.66
  8.1 20.0 %all-to-all-start = ((bf16[96,2,1408]{2,1,0:T(2,128)(2,1)}), bf16[96,2,1408]{2,1,0:T(2,128)(2,1)S(1)}, u32[]{:S(2)}, u32[]{:S(2)}) async-start(bf16[96,2,1408]{2,1,0:T(2,128)(2,1)} %reshape.66), calls=%async_computation | async-start | bytes 1081344 | tf_op jit(solution)/shard_map/all_to_all | solution.py:46
  28.2 0.4 reshape.63
  28.5 25.4 %all-to-all-done = bf16[96,2,1408]{2,1,0:T(2,128)(2,1)S(1)} async-done(((bf16[96,2,1408]{2,1,0:T(2,128)(2,1)}), bf16[96,2,1408]{2,1,0:T(2,128)(2,1)S(1)}, u32[]{:S(2)}, u32[]{:S(2)}) %all-to-all-start) | async-done | bytes 540704 | tf_op jit(solution)/shard_map/all_to_all | solution.py:46
  54.0 0.4 reshape.67
  54.4 1.0 convert_reduce_fusion
  55.5 0.3 broadcast_in_dim.65
  55.8 28.3 %all_to_all.35 = f32[48,1,2816]{2,1,0:T(1,128)S(1)} all-to-all(f32[48,1,2816]{2,1,0:T(1,128)S(1)} %broadcast_in_dim.65), channel_id=1, replica_groups=mesh['chip'=48,'core'=2,'zero'=8] {'chip'}, dimensions={0} | all-to-all | bytes 1081344 | tf_op jit(solution)/shard_map/all_to_all | solution.py:52
  84.1 4.8 %collective-permute-start = (f32[48,2816]{1,0:T(8,128)S(1)}, f32[48,2816]{1,0:T(8,128)S(1)}, u32[]{:S(2)}, u32[]{:S(2)}) collective-permute-start(f32[48,2816]{1,0:T(8,128)S(1)} %bitcast.28), channel_id=1, source_target_pairs={{0,8},{8,0},{1,9},{9,1},{2,10},{10,2},{3,11},{11,3},{4,12},{12,4},... | collective-permute-start | bytes 1622024 | tf_op jit(solution)/shard_map/ppermute | solution.py:53
  88.9 0.6 fusion.6
  89.6 0.6 iota_compare_fusion.2
  90.2 1.3 iota_compare_fusion
  91.5 0.0 collective-permute-done
  91.5 0.4 stack.8
  91.9 1.5 maximum_select_fusion.2
  93.4 0.9 select_n.85
  94.3 0.0 copy-start
  94.3 0.2 multiply_reduce_fusion
  94.5 0.7 broadcast_in_dim.67
  95.2 6.8 %all-to-all-start.2 = ((f32[8,1,3]{2,1,0:T(1,128)}), f32[8,1,3]{2,1,0:T(1,128)S(1)}, u32[]{:S(2)}, u32[]{:S(2)}) async-start(f32[8,1,3]{2,1,0:T(1,128)} %broadcast_in_dim.67), calls=%async_computation.2 | async-start | bytes 8192 | tf_op jit(solution)/shard_map/all_to_all | solution.py:59
  102.1 6.5 %all-to-all-done.2 = f32[8,1,3]{2,1,0:T(1,128)S(1)} async-done(((f32[8,1,3]{2,1,0:T(1,128)}), f32[8,1,3]{2,1,0:T(1,128)S(1)}, u32[]{:S(2)}, u32[]{:S(2)}) %all-to-all-start.2) | async-done | bytes 128 | tf_op jit(solution)/shard_map/all_to_all | solution.py:59
  108.6 0.2 multiply_convert_fusion.1
  108.9 0.2 select_select_fusion
  109.0 14.7 %all_to_all.36 = bf16[8,88,256]{2,1,0:T(8,128)(2,1)S(1)} all-to-all(bf16[8,88,256]{2,1,0:T(8,128)(2,1)S(1)} %select_select_fusion), channel_id=1, replica_groups=mesh['chip'=48,'core'=2,'zero'=8] {'zero'}, dimensions={0} | all-to-all | bytes 720896 | tf_op jit(solution)/shard_map/all_to_all | solution.py:83
  123.7 2.5 %collective-permute-start.1 = (bf16[8,88,256]{2,1,0:T(8,128)(2,1)S(1)}, bf16[8,88,256]{2,1,0:T(8,128)(2,1)S(1)}, u32[]{:S(2)}, u32[]{:S(2)}) collective-permute-start(bf16[8,88,256]{2,1,0:T(8,128)(2,1)S(1)} %all_to_all.36), channel_id=1, source_target_pairs={{0,16},{16,0},{32,48},{48,32},{64,80},{80,64},{96,112},{112,96},{1... | collective-permute-start | bytes 1081352 | tf_op jit(solution)/shard_map/ppermute | solution.py:72
  126.2 6.7 %collective-permute-done.1 = bf16[8,88,256]{2,1,0:T(8,128)(2,1)S(1)} collective-permute-done((bf16[8,88,256]{2,1,0:T(8,128)(2,1)S(1)}, bf16[8,88,256]{2,1,0:T(8,128)(2,1)S(1)}, u32[]{:S(2)}, u32[]{:S(2)}) %collective-permute-start.1) | collective-permute-done | bytes 360480 | tf_op jit(solution)/shard_map/ppermute | solution.py:72
  133.0 0.2 maximum_select_fusion.4
  133.1 5.4 %collective-permute-start.2 = (bf16[8,88,512]{2,1,0:T(8,128)(2,1)S(1)}, bf16[8,88,512]{2,1,0:T(8,128)(2,1)S(1)}, u32[]{:S(2)}, u32[]{:S(2)}) collective-permute-start(bf16[8,88,512]{2,1,0:T(8,128)(2,1)S(1)} %maximum_select_fusion.4), channel_id=1, source_target_pairs={{0,8},{8,0},{1,9},{9,1},{2,10},{10,2},{3,11},{11,3},{4,12},{12,4},... | collective-permute-start | bytes 2162696 | tf_op jit(solution)/shard_map/ppermute | solution.py:75
  138.5 0.2 maximum_select_fusion.3
  138.7 1.6 collective-permute-done.2
  140.3 1.3 convolution_convert_fusion.1
  141.7 3.3 %add_convert_fusion = bf16[704,1024]{1,0:T(8,128)(2,1)} fusion(bf16[704,704]{1,0:T(8,128)(2,1)S(1)} %convolution_convert_fusion.1, bf16[704,512]{1,0:T(8,128)(2,1)S(1)} %maximum_select_fusion.3, bf16[704,512]{1,0:T(8,128)(2,1)S(1)} %bitcast.32, pred[]{:T(512)S(6)} %eq.46), kind=kOutput, calls=%fused_computation.1 | convolution fusion | flops 1731186688 | bytes 3874817 | tf_op jit(solution)/shard_map/dot_general | solution.py:31
  145.0 4.4 %convolution_convert_fusion = bf16[704,704]{1,0:T(8,128)(2,1)} fusion(bf16[704,1024]{1,0:T(8,128)(2,1)} %add_convert_fusion), kind=kOutput, calls=%fused_computation.4 | convolution fusion | flops 1015517184 | bytes 2433024 | tf_op jit(solution)/shard_map/dot_general | solution.py:24
  149.4 4.3 %multiply_convert_fusion = bf16[704,1024]{1,0:T(8,128)(2,1)S(1)} fusion(bf16[704,1024]{1,0:T(8,128)(2,1)S(1)} %copy-done.4, bf16[704,704]{1,0:T(8,128)(2,1)} %convolution_convert_fusion), kind=kOutput, calls=%fused_computation | convolution fusion | flops 1718931456 | bytes 3874816 | tf_op jit(solution)/shard_map/dot_general | solution.py:31
  153.7 0.0 copy-start.2
  153.7 0.1 constant_dynamic-slice_fusion.5
  153.7 15.9 %all_to_all.37 = bf16[8,88,256]{2,1,0:T(8,128)(2,1)S(1)} all-to-all(bf16[8,88,256]{2,1,0:T(8,128)(2,1)S(1)} %constant_dynamic-slice_fusion.5), channel_id=1, replica_groups=mesh['chip'=48,'core'=2,'zero'=8] {'zero'}, dimensions={0} | all-to-all | bytes 720896 | tf_op jit(solution)/shard_map/all_to_all | solution.py:86
  169.6 2.5 %collective-permute-start.3 = (bf16[8,88,256]{2,1,0:T(8,128)(2,1)S(1)}, bf16[8,88,256]{2,1,0:T(8,128)(2,1)S(1)}, u32[]{:S(2)}, u32[]{:S(2)}) collective-permute-start(bf16[8,88,256]{2,1,0:T(8,128)(2,1)S(1)} %all_to_all.37), channel_id=1, source_target_pairs={{0,16},{16,0},{32,48},{48,32},{64,80},{80,64},{96,112},{112,96},{1... | collective-permute-start | bytes 1081352 | tf_op jit(solution)/shard_map/ppermute | solution.py:72
  172.1 7.5 %collective-permute-done.3 = bf16[8,88,256]{2,1,0:T(8,128)(2,1)S(1)} collective-permute-done((bf16[8,88,256]{2,1,0:T(8,128)(2,1)S(1)}, bf16[8,88,256]{2,1,0:T(8,128)(2,1)S(1)}, u32[]{:S(2)}, u32[]{:S(2)}) %collective-permute-start.3) | collective-permute-done | bytes 360480 | tf_op jit(solution)/shard_map/ppermute | solution.py:72
  179.6 0.2 maximum_select_fusion.5
  179.8 4.6 %collective-permute-start.4 = (bf16[8,88,512]{2,1,0:T(8,128)(2,1)S(1)}, bf16[8,88,512]{2,1,0:T(8,128)(2,1)S(1)}, u32[]{:S(2)}, u32[]{:S(2)}) collective-permute-start(bf16[8,88,512]{2,1,0:T(8,128)(2,1)S(1)} %maximum_select_fusion.5), channel_id=1, source_target_pairs={{0,8},{8,0},{1,9},{9,1},{2,10},{10,2},{3,11},{11,3},{4,12},{12,4},... | collective-permute-start | bytes 2162696 | tf_op jit(solution)/shard_map/ppermute | solution.py:75
  190.0 0.0 collective-permute-done.4
  190.0 0.4 maximum_select_fusion.1
  190.5 0.9 pad_maximum_fusion
  (15 shorter events, 0.3 us)
Async XLA Ops:
  7.2 21.0 %copy-start.1 = (f32[3,88,1024]{2,1,0:T(8,128)S(1)}, f32[3,88,1024]{2,1,0:T(8,128)}, u32[]{:S(2)}) copy-start(f32[3,88,1024]{2,1,0:T(8,128)} %param.4) | copy-start | bytes 3244036
  8.1 45.9 %all-to-all-start = ((bf16[96,2,1408]{2,1,0:T(2,128)(2,1)}), bf16[96,2,1408]{2,1,0:T(2,128)(2,1)S(1)}, u32[]{:S(2)}, u32[]{:S(2)}) async-start(bf16[96,2,1408]{2,1,0:T(2,128)(2,1)} %reshape.66), calls=%async_computation | async-start | bytes 1081344 | tf_op jit(solution)/shard_map/all_to_all | solution.py:46
  55.5 33.5 %copy-start.3 = (s32[3]{0:T(128)S(1)}, s32[3]{0:T(128)}, u32[]{:S(2)}) copy-start(s32[3]{0:T(128)} %param.5) | copy-start | bytes 40
  84.1 7.4 %collective-permute-start = (f32[48,2816]{1,0:T(8,128)S(1)}, f32[48,2816]{1,0:T(8,128)S(1)}, u32[]{:S(2)}, u32[]{:S(2)}) collective-permute-start(f32[48,2816]{1,0:T(8,128)S(1)} %bitcast.28), channel_id=1, source_target_pairs={{0,8},{8,0},{1,9},{9,1},{2,10},{10,2},{3,11},{11,3},{4,12},{12,4},... | collective-permute-start | bytes 1622024 | tf_op jit(solution)/shard_map/ppermute | solution.py:53
  94.3 14.5 %copy-start = (f32[3,88,1024]{2,1,0:T(8,128)}, f32[3,88,1024]{2,1,0:T(8,128)S(1)}, u32[]{:S(2)}) copy-start(f32[3,88,1024]{2,1,0:T(8,128)S(1)} %select_n.85) | copy-start | bytes 3244036
  95.2 13.3 %all-to-all-start.2 = ((f32[8,1,3]{2,1,0:T(1,128)}), f32[8,1,3]{2,1,0:T(1,128)S(1)}, u32[]{:S(2)}, u32[]{:S(2)}) async-start(f32[8,1,3]{2,1,0:T(1,128)} %broadcast_in_dim.67), calls=%async_computation.2 | async-start | bytes 8192 | tf_op jit(solution)/shard_map/all_to_all | solution.py:59
  123.7 9.2 %collective-permute-start.1 = (bf16[8,88,256]{2,1,0:T(8,128)(2,1)S(1)}, bf16[8,88,256]{2,1,0:T(8,128)(2,1)S(1)}, u32[]{:S(2)}, u32[]{:S(2)}) collective-permute-start(bf16[8,88,256]{2,1,0:T(8,128)(2,1)S(1)} %all_to_all.36), channel_id=1, source_target_pairs={{0,16},{16,0},{32,48},{48,32},{64,80},{80,64},{96,112},{112,96},{1... | collective-permute-start | bytes 1081352 | tf_op jit(solution)/shard_map/ppermute | solution.py:72
  133.1 7.2 %collective-permute-start.2 = (bf16[8,88,512]{2,1,0:T(8,128)(2,1)S(1)}, bf16[8,88,512]{2,1,0:T(8,128)(2,1)S(1)}, u32[]{:S(2)}, u32[]{:S(2)}) collective-permute-start(bf16[8,88,512]{2,1,0:T(8,128)(2,1)S(1)} %maximum_select_fusion.4), channel_id=1, source_target_pairs={{0,8},{8,0},{1,9},{9,1},{2,10},{10,2},{3,11},{11,3},{4,12},{12,4},... | collective-permute-start | bytes 2162696 | tf_op jit(solution)/shard_map/ppermute | solution.py:75
  145.0 4.4 %copy-start.4 = (bf16[704,1024]{1,0:T(8,128)(2,1)S(1)}, bf16[704,1024]{1,0:T(8,128)(2,1)}, u32[]{:S(2)}) copy-start(bf16[704,1024]{1,0:T(8,128)(2,1)} %add_convert_fusion) | copy-start | bytes 4325380
  153.7 26.1 %copy-start.2 = (bf16[704,1024]{1,0:T(8,128)(2,1)}, bf16[704,1024]{1,0:T(8,128)(2,1)S(1)}, u32[]{:S(2)}) copy-start(bf16[704,1024]{1,0:T(8,128)(2,1)S(1)} %multiply_convert_fusion) | copy-start | bytes 4325380
  169.6 10.0 %collective-permute-start.3 = (bf16[8,88,256]{2,1,0:T(8,128)(2,1)S(1)}, bf16[8,88,256]{2,1,0:T(8,128)(2,1)S(1)}, u32[]{:S(2)}, u32[]{:S(2)}) collective-permute-start(bf16[8,88,256]{2,1,0:T(8,128)(2,1)S(1)} %all_to_all.37), channel_id=1, source_target_pairs={{0,16},{16,0},{32,48},{48,32},{64,80},{80,64},{96,112},{112,96},{1... | collective-permute-start | bytes 1081352 | tf_op jit(solution)/shard_map/ppermute | solution.py:72
  179.8 10.2 %collective-permute-start.4 = (bf16[8,88,512]{2,1,0:T(8,128)(2,1)S(1)}, bf16[8,88,512]{2,1,0:T(8,128)(2,1)S(1)}, u32[]{:S(2)}, u32[]{:S(2)}) collective-permute-start(bf16[8,88,512]{2,1,0:T(8,128)(2,1)S(1)} %maximum_select_fusion.5), channel_id=1, source_target_pairs={{0,8},{8,0},{1,9},{9,1},{2,10},{10,2},{3,11},{11,3},{4,12},{12,4},... | collective-permute-start | bytes 2162696 | tf_op jit(solution)/shard_map/ppermute | solution.py:75

commit v10 on v8

--- a/solution.py
+++ b/solution.py
@@ -70,11 +70,12 @@
         return jnp.where(core == 0, jnp.concatenate([mine, other], axis=2),
                          jnp.concatenate([other, mine], axis=2))
 
-    outgoing = jnp.zeros((n_zero,) + start_rows.shape[1:], start_rows.dtype)
+    half_rows = own_half(start_rows)
+    outgoing = jnp.zeros((n_zero,) + half_rows.shape[1:], half_rows.dtype)
     owners = jnp.arange(n_zero, dtype=owner_table.dtype)[:, None, None]
-    for j in range(start_rows.shape[0]):
-        outgoing = jnp.where(owners == owner_table[j], start_rows[j][None], outgoing)
-    incoming = both_halves(lax.all_to_all(own_half(outgoing), "zero", 0, 0, tiled=True))
+    for j in range(half_rows.shape[0]):
+        outgoing = jnp.where(owners == owner_table[j], half_rows[j][None], outgoing)
+    incoming = both_halves(lax.all_to_all(outgoing, "zero", 0, 0, tiled=True))
     full_matrix = incoming.reshape(-1, incoming.shape[-1])
     result = orthogonalize(full_matrix)
     back = lax.all_to_all(own_half(result.reshape(incoming.shape)), "zero", 0, 0, tiled=True)

time: 186 us -> 186 us (level)
  no operation moved by 1% of the time
where the time goes in v10:
time: 186 us; the launch traced here: 185 us
  blocking collectives  75.1 us (40%)
  starting transfers between devices  38.7 us (21%)
  waiting for transfers between devices  33.7 us (18%)
  matrix products  12.2 us (7%)
  other arithmetic  10.3 us (6%)
  local copies, waits for them, and re-layouts  8.55 us (5%)
  between operations  6.54 us (4%)
    all_to_all x1, blocking collectives, on_device(): mine = lax.all_to_all(spread, 'chip', 0, 0, tiled=True)  28.3 us
    all_to_all x1, waiting for transfers between devices, on_device(): lax.all_to_all(local_part.reshape(n_dp, chunk), DP, 0, 0, tiled=True)  25.4 us
    all_to_all x1, blocking collectives, on_device(): lax.all_to_all(own_half(result.reshape(incoming.shape)), 'zero', 0, 0, ti...  24.6 us
    all_to_all x1, blocking collectives, on_device(): incoming = both_halves(lax.all_to_all(outgoing, 'zero', 0, 0, tiled=True))  22.3 us
    all_to_all x1, starting transfers between devices, on_device(): lax.all_to_all(local_part.reshape(n_dp, chunk), DP, 0, 0, tiled=True)  20 us
    dot_general x2, matrix products, orthogonalize(): jnp.dot(poly_term, current, preferred_element_type=jnp.float32)  8.59 us
    ppermute x2, starting transfers between devices, both_halves(): other = lax.ppermute(mine, 'core', [(0, 1), (1, 0)])  7.08 us
    all_to_all x1, starting transfers between devices, on_device(): lax.all_to_all(spread_sums, 'zero', 0, 0, tiled=True)  6.82 us
  transfers between devices with their start and end apart: 5, of which 3 were waited for; matrix products, arithmetic and copies ran while one was open for 2% of the time, Pallas kernels for 0%

profile of v10, /device:TPU:1, one launch (start us, length us, event | category | flops | bytes accessed | tf_op | source)
XLA Modules:
  0.0 185.1 jit_solution(8886620009364486108)
XLA Ops:
  0.6 2.1 %all_to_all.29 = bf16[96,1,2816]{2,1,0:T(2,128)(2,1)S(1)} reshape(bf16[1,3,88,1024]{3,2,1,0:T(8,128)(2,1)} %param.3) | data formatting | bytes 1081344 | tf_op jit(solution)/shard_map/all_to_all | solution.py:46
  2.8 0.5 broadcast.71
  3.3 3.9 %reduce.4 = bf16[96,2816]{1,0:T(8,128)(2,1)S(1)} reduce(bf16[96,1,2816]{2,1,0:T(2,128)(2,1)S(1)} %all_to_all.29, bf16[]{:T(256)} %broadcast.71), dimensions={1}, to_apply=%all_to_all.29.reduce_sub_computation | reduce | bytes 1081346 | tf_op jit(solution)/shard_map/all_to_all | solution.py:46
  7.2 0.0 copy-start.1
  7.2 0.9 reshape.62
  8.1 20.0 %all-to-all-start = ((bf16[96,2,1408]{2,1,0:T(2,128)(2,1)}), bf16[96,2,1408]{2,1,0:T(2,128)(2,1)S(1)}, u32[]{:S(2)}, u32[]{:S(2)}) async-start(bf16[96,2,1408]{2,1,0:T(2,128)(2,1)} %reshape.62), calls=%async_computation | async-start | bytes 1081344 | tf_op jit(solution)/shard_map/all_to_all | solution.py:46
  28.1 0.0 copy-done.1
  28.2 0.4 reshape.59
  28.5 25.4 %all-to-all-done = bf16[96,2,1408]{2,1,0:T(2,128)(2,1)S(1)} async-done(((bf16[96,2,1408]{2,1,0:T(2,128)(2,1)}), bf16[96,2,1408]{2,1,0:T(2,128)(2,1)S(1)}, u32[]{:S(2)}, u32[]{:S(2)}) %all-to-all-start) | async-done | bytes 540704 | tf_op jit(solution)/shard_map/all_to_all | solution.py:46
  54.0 0.4 reshape.63
  54.4 1.0 convert_reduce_fusion
  55.5 0.0 copy-start.3
  55.5 0.3 broadcast_in_dim.65
  55.8 28.3 %all_to_all.35 = f32[48,1,2816]{2,1,0:T(1,128)S(1)} all-to-all(f32[48,1,2816]{2,1,0:T(1,128)S(1)} %broadcast_in_dim.65), channel_id=1, replica_groups=mesh['chip'=48,'core'=2,'zero'=8] {'chip'}, dimensions={0} | all-to-all | bytes 1081344 | tf_op jit(solution)/shard_map/all_to_all | solution.py:52
  84.1 4.8 %collective-permute-start = (f32[48,2816]{1,0:T(8,128)S(1)}, f32[48,2816]{1,0:T(8,128)S(1)}, u32[]{:S(2)}, u32[]{:S(2)}) collective-permute-start(f32[48,2816]{1,0:T(8,128)S(1)} %bitcast.27), channel_id=1, source_target_pairs={{0,8},{8,0},{1,9},{9,1},{2,10},{10,2},{3,11},{11,3},{4,12},{12,4},... | collective-permute-start | bytes 1622024 | tf_op jit(solution)/shard_map/ppermute | solution.py:53
  88.9 0.0 copy-done.3
  88.9 0.6 fusion.7
  89.5 0.6 iota_compare_fusion.2
  90.2 1.2 iota_compare_fusion
  91.4 0.0 collective-permute-done
  91.4 0.4 stack.8
  91.8 1.5 maximum_select_fusion.2
  93.4 0.9 select_n.57
  94.2 0.0 copy-start
  94.3 0.2 multiply_reduce_fusion
  94.5 0.7 broadcast_in_dim.67
  95.2 6.8 %all-to-all-start.2 = ((f32[8,1,3]{2,1,0:T(1,128)}), f32[8,1,3]{2,1,0:T(1,128)S(1)}, u32[]{:S(2)}, u32[]{:S(2)}) async-start(f32[8,1,3]{2,1,0:T(1,128)} %broadcast_in_dim.67), calls=%async_computation.2 | async-start | bytes 8192 | tf_op jit(solution)/shard_map/all_to_all | solution.py:59
  102.0 6.5 %all-to-all-done.2 = f32[8,1,3]{2,1,0:T(1,128)S(1)} async-done(((f32[8,1,3]{2,1,0:T(1,128)}), f32[8,1,3]{2,1,0:T(1,128)S(1)}, u32[]{:S(2)}, u32[]{:S(2)}) %all-to-all-start.2) | async-done | bytes 128 | tf_op jit(solution)/shard_map/all_to_all | solution.py:59
  108.5 0.1 fusion
  108.7 0.3 select_select_fusion
  109.0 0.0 copy-done
  109.0 22.3 %all_to_all.36 = bf16[8,88,512]{2,1,0:T(8,128)(2,1)S(1)} all-to-all(bf16[8,88,512]{2,1,0:T(8,128)(2,1)S(1)} %select_select_fusion), channel_id=1, replica_groups=mesh['chip'=48,'core'=2,'zero'=8] {'zero'}, dimensions={0} | all-to-all | bytes 1441792 | tf_op jit(solution)/shard_map/all_to_all | solution.py:78
  131.3 4.7 %collective-permute-start.1 = (bf16[8,88,512]{2,1,0:T(8,128)(2,1)S(1)}, bf16[8,88,512]{2,1,0:T(8,128)(2,1)S(1)}, u32[]{:S(2)}, u32[]{:S(2)}) collective-permute-start(bf16[8,88,512]{2,1,0:T(8,128)(2,1)S(1)} %all_to_all.36), channel_id=1, source_target_pairs={{0,8},{8,0},{1,9},{9,1},{2,10},{10,2},{3,11},{11,3},{4,12},{12,4},... | collective-permute-start | bytes 2162696 | tf_op jit(solution)/shard_map/ppermute | solution.py:69
  135.9 1.8 collective-permute-done.1
  137.7 2.3 %convolution_convert_fusion.1 = bf16[704,704]{1,0:T(8,128)(2,1)} fusion(bf16[704,512]{1,0:T(8,128)(2,1)S(1)} %bitcast.30, bf16[704,512]{1,0:T(8,128)(2,1)S(1)} %bitcast.25, pred[]{:T(512)S(6)} %eq.38), kind=kOutput, calls=%fused_computation.5 | convolution fusion | flops 1022005248 | bytes 2433025 | tf_op jit(solution)/shard_map/dot_general | solution.py:24
  140.1 4.5 %add_convert_fusion = bf16[704,1024]{1,0:T(8,128)(2,1)S(1)} fusion(bf16[704,704]{1,0:T(8,128)(2,1)} %convolution_convert_fusion.1, bf16[704,512]{1,0:T(8,128)(2,1)S(1)} %bitcast.26, bf16[704,512]{1,0:T(8,128)(2,1)S(1)} %bitcast.31, pred[]{:T(512)S(6)} %eq.38), kind=kOutput, calls=%fused_computation.1 | convolution fusion | flops 1731186688 | bytes 3874817 | tf_op jit(solution)/shard_map/dot_general | solution.py:31
  144.6 0.0 copy-start.4
  144.6 1.1 copy-done.4
  145.7 1.3 convolution_convert_fusion
  147.0 4.1 %multiply_convert_fusion = bf16[704,1024]{1,0:T(8,128)(2,1)S(1)} fusion(bf16[704,1024]{1,0:T(8,128)(2,1)} %copy-done.4, bf16[704,704]{1,0:T(8,128)(2,1)S(1)} %convolution_convert_fusion), kind=kOutput, calls=%fused_computation | convolution fusion | flops 1718931456 | bytes 3874816 | tf_op jit(solution)/shard_map/dot_general | solution.py:31
  151.1 0.0 copy-start.2
  151.1 0.1 constant_dynamic-slice_fusion.3
  151.2 24.6 %all_to_all.37 = bf16[8,88,512]{2,1,0:T(8,128)(2,1)S(1)} all-to-all(bf16[8,88,512]{2,1,0:T(8,128)(2,1)S(1)} %constant_dynamic-slice_fusion.3), channel_id=1, replica_groups=mesh['chip'=48,'core'=2,'zero'=8] {'zero'}, dimensions={0} | all-to-all | bytes 1441792 | tf_op jit(solution)/shard_map/all_to_all | solution.py:81
  175.8 0.0 copy-done.2
  175.8 2.4 %collective-permute-start.2 = (bf16[8,88,512]{2,1,0:T(8,128)(2,1)S(1)}, bf16[8,88,512]{2,1,0:T(8,128)(2,1)S(1)}, u32[]{:S(2)}, u32[]{:S(2)}) collective-permute-start(bf16[8,88,512]{2,1,0:T(8,128)(2,1)S(1)} %all_to_all.37), channel_id=1, source_target_pairs={{0,8},{8,0},{1,9},{9,1},{2,10},{10,2},{3,11},{11,3},{4,12},{12,4},... | collective-permute-start | bytes 2162696 | tf_op jit(solution)/shard_map/ppermute | solution.py:69
  183.8 0.0 collective-permute-done.2
  183.8 0.4 maximum_select_fusion.1
  184.3 0.9 pad_maximum_fusion
  (6 shorter events, 0.2 us)
Async XLA Ops:
  7.2 21.0 %copy-start.1 = (f32[3,88,1024]{2,1,0:T(8,128)S(1)}, f32[3,88,1024]{2,1,0:T(8,128)}, u32[]{:S(2)}) copy-start(f32[3,88,1024]{2,1,0:T(8,128)} %param.4) | copy-start | bytes 3244036
  8.1 45.9 %all-to-all-start = ((bf16[96,2,1408]{2,1,0:T(2,128)(2,1)}), bf16[96,2,1408]{2,1,0:T(2,128)(2,1)S(1)}, u32[]{:S(2)}, u32[]{:S(2)}) async-start(bf16[96,2,1408]{2,1,0:T(2,128)(2,1)} %reshape.62), calls=%async_computation | async-start | bytes 1081344 | tf_op jit(solution)/shard_map/all_to_all | solution.py:46
  55.5 33.4 %copy-start.3 = (s32[3]{0:T(128)S(1)}, s32[3]{0:T(128)}, u32[]{:S(2)}) copy-start(s32[3]{0:T(128)} %param.5) | copy-start | bytes 40
  84.1 7.3 %collective-permute-start = (f32[48,2816]{1,0:T(8,128)S(1)}, f32[48,2816]{1,0:T(8,128)S(1)}, u32[]{:S(2)}, u32[]{:S(2)}) collective-permute-start(f32[48,2816]{1,0:T(8,128)S(1)} %bitcast.27), channel_id=1, source_target_pairs={{0,8},{8,0},{1,9},{9,1},{2,10},{10,2},{3,11},{11,3},{4,12},{12,4},... | collective-permute-start | bytes 1622024 | tf_op jit(solution)/shard_map/ppermute | solution.py:53
  94.2 14.7 %copy-start = (f32[3,88,1024]{2,1,0:T(8,128)}, f32[3,88,1024]{2,1,0:T(8,128)S(1)}, u32[]{:S(2)}) copy-start(f32[3,88,1024]{2,1,0:T(8,128)S(1)} %select_n.57) | copy-start | bytes 3244036
  95.2 13.3 %all-to-all-start.2 = ((f32[8,1,3]{2,1,0:T(1,128)}), f32[8,1,3]{2,1,0:T(1,128)S(1)}, u32[]{:S(2)}, u32[]{:S(2)}) async-start(f32[8,1,3]{2,1,0:T(1,128)} %broadcast_in_dim.67), calls=%async_computation.2 | async-start | bytes 8192 | tf_op jit(solution)/shard_map/all_to_all | solution.py:59
  131.3 6.5 %collective-permute-start.1 = (bf16[8,88,512]{2,1,0:T(8,128)(2,1)S(1)}, bf16[8,88,512]{2,1,0:T(8,128)(2,1)S(1)}, u32[]{:S(2)}, u32[]{:S(2)}) collective-permute-start(bf16[8,88,512]{2,1,0:T(8,128)(2,1)S(1)} %all_to_all.36), channel_id=1, source_target_pairs={{0,8},{8,0},{1,9},{9,1},{2,10},{10,2},{3,11},{11,3},{4,12},{12,4},... | collective-permute-start | bytes 2162696 | tf_op jit(solution)/shard_map/ppermute | solution.py:69
  144.6 1.1 copy-start.4
  151.1 24.7 %copy-start.2 = (bf16[704,1024]{1,0:T(8,128)(2,1)}, bf16[704,1024]{1,0:T(8,128)(2,1)S(1)}, u32[]{:S(2)}) copy-start(bf16[704,1024]{1,0:T(8,128)(2,1)S(1)} %multiply_convert_fusion) | copy-start | bytes 4325380
  175.8 8.0 %collective-permute-start.2 = (bf16[8,88,512]{2,1,0:T(8,128)(2,1)S(1)}, bf16[8,88,512]{2,1,0:T(8,128)(2,1)S(1)}, u32[]{:S(2)}, u32[]{:S(2)}) collective-permute-start(bf16[8,88,512]{2,1,0:T(8,128)(2,1)S(1)} %all_to_all.37), channel_id=1, source_target_pairs={{0,8},{8,0},{1,9},{9,1},{2,10},{10,2},{3,11},{11,3},{4,12},{12,4},... | collective-permute-start | bytes 2162696 | tf_op jit(solution)/shard_map/ppermute | solution.py:69
